TPU v7x, 32 devices: a whole 2x2x4 slice. The times are simulated.
32 devices in a mesh: seq: 8 (over y, x, core), head: 4 (over z).
Axes of the slice: x: 2, y: 2, z: 4, core: 2. Of those that a mesh axis runs over, the one named last changes fastest.
Arguments:
- query_rows: bfloat16 [4096, 8192], P(('seq', 'head')), may hold values from -150 to 150
- key_rows: bfloat16 [4096, 1024], P(('seq', 'head')), may hold values from -5 to 5
- value_rows: bfloat16 [4096, 1024], P(('seq', 'head')), may hold values from -6 to 6
- doc_ids: int32 [4096], replicated, may hold values from 0 to 1, never falling along the last dimension, each value on 1 to 3584 neighbouring positions
Outputs:
- attended: bfloat16 [4096, 8192], P(('seq', 'head'))
Inputs may be any that keep to these rules, and one draw needn't show every extreme that they name: `doc_ids`: never falls along the pack; each document has 1 to 3584 tokens.
All inputs are finite; a program needn't handle non-finite values.
Results may differ from a plain program's by a relative error of at most 0.0039.
Values may be sent and summed in bfloat16 or wider, within the bound.
No kernel may reach another device: no remote copies, remote signals or barrier semaphores. Data moves between devices by JAX's collectives and lax.ppermute only.
A program may use at most 128 MiB of HBM per device.

v0:
```python
import functools
import math

import jax
import jax.numpy as jnp
from jax import lax
from jax.experimental import pallas as pl
from jax.experimental.pallas import tpu as pltpu
from jax.sharding import PartitionSpec as P

HEAD_DIM = 128
KEY_ROWS = 512
DOC_MOST = 3584
NEG_START = -1e30


def flash_kernel(meta_ref, doc_ref, q_ref, k_ref, v_ref, qstart_ref, o_ref, qt_sc, m_sc, l_sc, acc_sc,
                 *, heads_per, groups, q_rows, steps, scale):
    step = pl.program_id(0)
    first_block = meta_ref[0]
    last_block = meta_ref[1]
    q_off = meta_ref[2]
    key_block = jnp.minimum(first_block + step, last_block)
    active = first_block + step <= last_block
    full = (key_block * KEY_ROWS + KEY_ROWS - 1 < q_off) & (
        doc_ref[key_block * KEY_ROWS] == doc_ref[q_off + q_rows - 1]
    )

    @pl.when(step == 0)
    def _():
        m_sc[...] = jnp.full(m_sc.shape, NEG_START, jnp.float32)
        l_sc[...] = jnp.zeros(l_sc.shape, jnp.float32)
        acc_sc[...] = jnp.zeros(acc_sc.shape, jnp.float32)
        for j in range(groups * heads_per):
            cols = slice(j * HEAD_DIM, (j + 1) * HEAD_DIM)
            qt_sc[j] = q_ref[:, cols].astype(jnp.float32).T.astype(jnp.bfloat16)

    def compute(masked):
        if masked:
            key_pos = key_block * KEY_ROWS + lax.broadcasted_iota(jnp.int32, (KEY_ROWS, q_rows), 0)
            query_pos = q_off + lax.broadcasted_iota(jnp.int32, (KEY_ROWS, q_rows), 1)
            visible = (key_pos <= query_pos) & (key_pos >= qstart_ref[...])
        for g in range(groups):
            keys = k_ref[:, g * HEAD_DIM:(g + 1) * HEAD_DIM]
            values_t = v_ref[:, g * HEAD_DIM:(g + 1) * HEAD_DIM].T
            for r in range(heads_per):
                j = g * heads_per + r
                scores = jnp.dot(keys, qt_sc[j], preferred_element_type=jnp.float32)
                if masked:
                    scores = jnp.where(visible, scores, -jnp.inf)
                m_old = m_sc[j]
                m_new = jnp.maximum(m_old, jnp.max(scores, axis=0, keepdims=True))
                weights = jnp.exp2((scores - m_new) * scale)
                factor = jnp.exp2((m_old - m_new) * scale)
                l_sc[j] = l_sc[j] * factor + jnp.sum(weights, axis=0, keepdims=True)
                product = jnp.dot(values_t, weights.astype(jnp.bfloat16), preferred_element_type=jnp.float32)
                acc_sc[j] = acc_sc[j] * factor + product
                m_sc[j] = m_new

    @pl.when(active & full)
    def _():
        compute(False)

    @pl.when(active & jnp.logical_not(full))
    def _():
        compute(True)

    @pl.when(step == steps - 1)
    def _():
        for j in range(groups * heads_per):
            cols = slice(j * HEAD_DIM, (j + 1) * HEAD_DIM)
            o_ref[:, cols] = (acc_sc[j] / l_sc[j]).T.astype(o_ref.dtype)


def attend(q_tile, q_off, kv_rows, doc_ids, groups, heads_per):
    tokens = doc_ids.shape[0]
    q_rows = q_tile.shape[0]
    blocks = tokens // KEY_ROWS
    steps = min(blocks, -(-DOC_MOST // KEY_ROWS) + 1)
    query_doc = lax.dynamic_slice_in_dim(doc_ids, q_off, q_rows)
    query_start = jnp.sum((doc_ids[None, :] < query_doc[:, None]).astype(jnp.int32), axis=1).reshape(1, q_rows)
    meta = jnp.stack([query_start[0, 0] // KEY_ROWS, (q_off + q_rows - 1) // KEY_ROWS, q_off]).astype(jnp.int32)
    width = groups * heads_per * HEAD_DIM
    kv_width = groups * HEAD_DIM
    heads = groups * heads_per

    def key_index(j, meta, docs):
        return jnp.minimum(meta[0] + j, meta[1])

    kernel = functools.partial(
        flash_kernel, heads_per=heads_per, groups=groups, q_rows=q_rows, steps=steps,
        scale=math.log2(math.e) / HEAD_DIM**0.5,
    )
    return pl.pallas_call(
        kernel,
        out_shape=jax.ShapeDtypeStruct((q_rows, width), jnp.bfloat16),
        grid_spec=pltpu.PrefetchScalarGridSpec(
            num_scalar_prefetch=2,
            grid=(steps,),
            in_specs=[
                pl.BlockSpec((q_rows, width), lambda j, meta, docs: (0, 0)),
                pl.BlockSpec((KEY_ROWS, kv_width), lambda j, meta, docs: (key_index(j, meta, docs), 0)),
                pl.BlockSpec((KEY_ROWS, kv_width), lambda j, meta, docs: (key_index(j, meta, docs), 1)),
                pl.BlockSpec((1, q_rows), lambda j, meta, docs: (0, 0)),
            ],
            out_specs=pl.BlockSpec((q_rows, width), lambda j, meta, docs: (0, 0)),
            scratch_shapes=[
                pltpu.VMEM((heads, HEAD_DIM, q_rows), jnp.bfloat16),
                pltpu.VMEM((heads, 1, q_rows), jnp.float32),
                pltpu.VMEM((heads, 1, q_rows), jnp.float32),
                pltpu.VMEM((heads, HEAD_DIM, q_rows), jnp.float32),
            ],
        ),
        compiler_params=pltpu.CompilerParams(dimension_semantics=("arbitrary",)),
    )(meta, doc_ids, q_tile, kv_rows, kv_rows, query_start)


def gather_kv(key_rows, value_rows):
    head_count = lax.axis_size("head")
    head = lax.axis_index("head")
    sub = key_rows.shape[0]
    width = key_rows.shape[1] // head_count
    local = jnp.zeros((head_count * sub, 2 * width), key_rows.dtype)
    for t in range(head_count):
        cols = ((head + t) % head_count) * width
        piece = jnp.concatenate(
            [lax.dynamic_slice_in_dim(key_rows, cols, width, axis=1),
             lax.dynamic_slice_in_dim(value_rows, cols, width, axis=1)], axis=1)
        if t:
            piece = lax.ppermute(piece, "head", [(i, (i + t) % head_count) for i in range(head_count)])
        local = lax.dynamic_update_slice_in_dim(local, piece, ((head - t) % head_count) * sub, axis=0)
    return lax.all_gather(local, "seq", axis=0, tiled=True)


def body(query_rows, key_rows, value_rows, doc_ids):
    head_count = lax.axis_size("head")
    head = lax.axis_index("head")
    sub = query_rows.shape[0]
    q_width = query_rows.shape[1] // head_count
    groups = key_rows.shape[1] // HEAD_DIM // head_count
    heads_per = query_rows.shape[1] // key_rows.shape[1]
    block_start = lax.axis_index("seq") * sub * head_count
    kv_rows = gather_kv(key_rows, value_rows)
    result = jnp.zeros_like(query_rows)
    for t in range(head_count):
        piece = lax.dynamic_slice_in_dim(query_rows, ((head + t) % head_count) * q_width, q_width, axis=1)
        if t:
            piece = lax.ppermute(piece, "head", [(i, (i + t) % head_count) for i in range(head_count)])
        q_off = block_start + ((head - t) % head_count) * sub
        out_tile = attend(piece, q_off, kv_rows, doc_ids, groups, heads_per)
        if t:
            out_tile = lax.ppermute(out_tile, "head", [(i, (i - t) % head_count) for i in range(head_count)])
        result = lax.dynamic_update_slice_in_dim(result, out_tile, ((head + t) % head_count) * q_width, axis=1)
    return result


def solution(mesh):
    placed = (P(("seq", "head"), None), P(("seq", "head"), None), P(("seq", "head"), None), P())
    return jax.shard_map(
        body, mesh=mesh, in_specs=placed, out_specs=P(("seq", "head"), None), check_vma=False
    )
```

profile of v0, /device:TPU:6, one launch (start us, length us, event | category | flops | bytes accessed | tf_op | source)
XLA Modules:
  0.0 132.0 jit_solution(14993690222506646179)
XLA Ops:
  6.5 0.0 all-gather.2.cloned.1.call-start
  6.5 1.3 constant_dynamic-slice_fusion.3
  7.8 1.6 %collective-permute-start = (bf16[128,512]{1,0:T(8,128)(2,1)S(1)}, bf16[128,512]{1,0:T(8,128)(2,1)S(1)}, u32[]{:S(2)}, u32[]{:S(2)}) collective-permute-start(bf16[128,512]{1,0:T(8,128)(2,1)S(1)} %pad_maximum_fusion), channel_id=1, source_target_pairs={{0,1},{1,2},{2,3},{3,0},{4,5},{5,6},{6,7},{7,4},{8,9},{9,10},{10,1... | collective-permute-start | bytes 393224 | tf_op jit(solution)/shard_map/ppermute | solution.py:130
  9.5 2.7 %collective-permute-start.1 = (bf16[128,512]{1,0:T(8,128)(2,1)S(1)}, bf16[128,512]{1,0:T(8,128)(2,1)S(1)}, u32[]{:S(2)}, u32[]{:S(2)}) collective-permute-start(bf16[128,512]{1,0:T(8,128)(2,1)S(1)} %pad_maximum_fusion.1), channel_id=1, source_target_pairs={{0,2},{1,3},{2,0},{3,1},{4,6},{5,7},{6,4},{7,5},{8,10},{9,11},{10,... | collective-permute-start | bytes 393224 | tf_op jit(solution)/shard_map/ppermute | solution.py:130
  12.1 1.4 %collective-permute-start.2 = (bf16[128,512]{1,0:T(8,128)(2,1)S(1)}, bf16[128,512]{1,0:T(8,128)(2,1)S(1)}, u32[]{:S(2)}, u32[]{:S(2)}) collective-permute-start(bf16[128,512]{1,0:T(8,128)(2,1)S(1)} %pad_maximum_fusion.2), channel_id=1, source_target_pairs={{0,3},{1,0},{2,1},{3,2},{4,7},{5,4},{6,5},{7,6},{8,11},{9,8},{10,9... | collective-permute-start | bytes 393224 | tf_op jit(solution)/shard_map/ppermute | solution.py:130
  13.7 2.5 %collective-permute-done = bf16[128,512]{1,0:T(8,128)(2,1)S(1)} collective-permute-done((bf16[128,512]{1,0:T(8,128)(2,1)S(1)}, bf16[128,512]{1,0:T(8,128)(2,1)S(1)}, u32[]{:S(2)}, u32[]{:S(2)}) %collective-permute-start) | collective-permute-done | bytes 131104 | tf_op jit(solution)/shard_map/ppermute | solution.py:130
  16.2 4.5 %collective-permute-done.1 = bf16[128,512]{1,0:T(8,128)(2,1)S(1)} collective-permute-done((bf16[128,512]{1,0:T(8,128)(2,1)S(1)}, bf16[128,512]{1,0:T(8,128)(2,1)S(1)}, u32[]{:S(2)}, u32[]{:S(2)}) %collective-permute-start.1) | collective-permute-done | bytes 131104 | tf_op jit(solution)/shard_map/ppermute | solution.py:130
  20.7 0.0 collective-permute-done.2
  20.7 0.0 copy-start.2
  20.7 0.8 copy-done.2
  21.5 0.0 all-gather.2.cloned.1.call-update
  21.6 0.0 copy-done.3
  21.6 0.0 copy-start.7
  21.6 1.2 constant_dynamic-slice_fusion
  22.8 3.2 %collective-permute-start.3 = (bf16[128,2048]{1,0:T(8,128)(2,1)}, bf16[128,2048]{1,0:T(8,128)(2,1)S(1)}, u32[]{:S(2)}, u32[]{:S(2)}) collective-permute-start(bf16[128,2048]{1,0:T(8,128)(2,1)} %get-tuple-element.10), channel_id=1, source_target_pairs={{0,1},{1,2},{2,3},{3,0},{4,5},{5,6},{6,7},{7,4},{8,9},{9,10},{10,1... | collective-permute-start | bytes 1572872 | tf_op jit(solution)/shard_map/ppermute | solution.py:148
  26.0 1.1 collective-permute-start.7
  27.1 0.6 collective-permute-start.5
  27.7 0.0 copy-done.7
  27.7 0.1 fusion
  27.8 1.0 convert_reduce_fusion
  28.8 0.0 copy-start.8
  28.8 0.0 copy-start.9
  29.5 0.7 pad_add_fusion.1.meta_ref
  30.2 10.0 %collective-permute-done.3.q_ref = bf16[128,2048]{1,0:T(8,128)(2,1)S(1)} collective-permute-done((bf16[128,2048]{1,0:T(8,128)(2,1)}, bf16[128,2048]{1,0:T(8,128)(2,1)S(1)}, u32[]{:S(2)}, u32[]{:S(2)}) %collective-permute-start.3) | collective-permute-done | bytes 524320 | tf_op jit(solution)/shard_map/ppermute | solution.py:148
  40.2 19.2 %all-gather.2.cloned.1.call-done.k_ref.v_ref = bf16[4096,512]{1,0:T(8,128)(2,1)} async-done(((bf16[512,512]{1,0:T(8,128)(2,1)}), bf16[4096,512]{1,0:T(8,128)(2,1)}) %all-gather.2.cloned.1.call-update) | async-done | bytes 4194320 | tf_op jit(solution)/shard_map/all_gather | solution.py:132
  59.5 10.7 %shard_map.47 = bf16[128,2048]{1,0:T(8,128)(2,1)} custom-call(s32[3]{0:T(128)} %pad_add_fusion.1.meta_ref, s32[4096]{0:T(1024)} %doc_ref.7, bf16[128,2048]{1,0:T(8,128)(2,1)} %copy-done.6, bf16[4096,512]{1,0:T(8,128)(2,1)} %all-gather.2.cloned.1.call-done.k_ref.v_ref, bf16[4096,512]{1,0:T(8,128)(2,1)} %all-gather.2.cloned.1.call-done.k_ref.v_ref, ...), custom_call_target="tpu_custom_call" | custom-call | tf_op jit(solution)/shard_map/pallas_call | solution.py:94
  70.2 0.0 copy-done.10
  70.2 3.6 %collective-permute-start.4 = (bf16[128,2048]{1,0:T(8,128)(2,1)}, bf16[128,2048]{1,0:T(8,128)(2,1)S(1)}, u32[]{:S(2)}, u32[]{:S(2)}) collective-permute-start(bf16[128,2048]{1,0:T(8,128)(2,1)} %shard_map.47), channel_id=1, source_target_pairs={{0,3},{1,0},{2,1},{3,2},{4,7},{5,4},{6,5},{7,6},{8,11},{9,8},{10,9... | collective-permute-start | bytes 1572872 | tf_op jit(solution)/shard_map/ppermute | solution.py:152
  73.8 0.6 pad_add_fusion.3.meta_ref
  74.4 0.6 pad_add_fusion.2.meta_ref
  75.0 0.0 collective-permute-done.5.q_ref
  75.0 0.8 copy-done.5
  75.8 10.8 %shard_map.48 = bf16[128,2048]{1,0:T(8,128)(2,1)} custom-call(s32[3]{0:T(128)} %pad_add_fusion.2.meta_ref, s32[4096]{0:T(1024)} %doc_ref.7, bf16[128,2048]{1,0:T(8,128)(2,1)} %copy-done.5, bf16[4096,512]{1,0:T(8,128)(2,1)} %all-gather.2.cloned.1.call-done.k_ref.v_ref, bf16[4096,512]{1,0:T(8,128)(2,1)} %all-gather.2.cloned.1.call-done.k_ref.v_ref, ...), custom_call_target="tpu_custom_call" | custom-call | tf_op jit(solution)/shard_map/pallas_call | solution.py:94
  86.6 0.0 collective-permute-start.6
  86.6 0.6 pad_add_fusion.meta_ref
  87.2 0.0 collective-permute-done.7.q_ref
  87.2 0.8 copy-done.4
  88.0 10.8 %shard_map.49 = bf16[128,2048]{1,0:T(8,128)(2,1)} custom-call(s32[3]{0:T(128)} %pad_add_fusion.3.meta_ref, s32[4096]{0:T(1024)} %doc_ref.7, bf16[128,2048]{1,0:T(8,128)(2,1)} %copy-done.4, bf16[4096,512]{1,0:T(8,128)(2,1)} %all-gather.2.cloned.1.call-done.k_ref.v_ref, bf16[4096,512]{1,0:T(8,128)(2,1)} %all-gather.2.cloned.1.call-done.k_ref.v_ref, ...), custom_call_target="tpu_custom_call" | custom-call | tf_op jit(solution)/shard_map/pallas_call | solution.py:94
  98.7 1.1 collective-permute-start.8
  99.8 10.7 %shard_map.46 = bf16[128,2048]{1,0:T(8,128)(2,1)} custom-call(s32[3]{0:T(128)} %pad_add_fusion.meta_ref, s32[4096]{0:T(1024)} %doc_ref.7, bf16[128,2048]{1,0:T(8,128)(2,1)} %get-tuple-element.11.q_ref, bf16[4096,512]{1,0:T(8,128)(2,1)} %all-gather.2.cloned.1.call-done.k_ref.v_ref, bf16[4096,512]{1,0:T(8,128)(2,1)} %all-gather.2.cloned.1.call-done.k_ref.v_ref, ...), custom_call_target="tpu_custom_call" | custom-call | tf_op jit(solution)/shard_map/pallas_call | solution.py:94
  110.6 0.2 broadcast_in_dim.4
  110.8 0.8 copy-done.1
  111.7 0.0 collective-permute-done.4
  111.7 11.2 %collective-permute-done.6 = bf16[128,2048]{1,0:T(8,128)(2,1)S(1)} collective-permute-done((bf16[128,2048]{1,0:T(8,128)(2,1)}, bf16[128,2048]{1,0:T(8,128)(2,1)S(1)}, u32[]{:S(2)}, u32[]{:S(2)}) %collective-permute-start.6) | collective-permute-done | bytes 524320 | tf_op jit(solution)/shard_map/ppermute | solution.py:152
  123.0 0.0 copy-start
  123.1 0.0 collective-permute-done.8
  123.1 1.3 copy-done
  124.4 0.8 constant_dynamic-update-slice_fusion
  (22 shorter events, 0.3 us)
Async XLA Ops:
  6.5 52.9 %all-gather.2.cloned.1.call-start = ((), (), s32[]{:S(2)}) async-start(), calls=%async_computation | async-start | bytes 4718592 | tf_op jit(solution)/shard_map/all_gather | solution.py:132
  6.5 15.1 %copy-start.3 = (bf16[128,8192]{1,0:T(8,128)(2,1)S(1)}, bf16[128,8192]{1,0:T(8,128)(2,1)}, u32[]{:S(2)}) copy-start(bf16[128,8192]{1,0:T(8,128)(2,1)} %param.4) | copy-start | bytes 6291460
  7.8 8.3 %collective-permute-start = (bf16[128,512]{1,0:T(8,128)(2,1)S(1)}, bf16[128,512]{1,0:T(8,128)(2,1)S(1)}, u32[]{:S(2)}, u32[]{:S(2)}) collective-permute-start(bf16[128,512]{1,0:T(8,128)(2,1)S(1)} %pad_maximum_fusion), channel_id=1, source_target_pairs={{0,1},{1,2},{2,3},{3,0},{4,5},{5,6},{6,7},{7,4},{8,9},{9,10},{10,1... | collective-permute-start | bytes 393224 | tf_op jit(solution)/shard_map/ppermute | solution.py:130
  9.5 11.2 %collective-permute-start.1 = (bf16[128,512]{1,0:T(8,128)(2,1)S(1)}, bf16[128,512]{1,0:T(8,128)(2,1)S(1)}, u32[]{:S(2)}, u32[]{:S(2)}) collective-permute-start(bf16[128,512]{1,0:T(8,128)(2,1)S(1)} %pad_maximum_fusion.1), channel_id=1, source_target_pairs={{0,2},{1,3},{2,0},{3,1},{4,6},{5,7},{6,4},{7,5},{8,10},{9,11},{10,... | collective-permute-start | bytes 393224 | tf_op jit(solution)/shard_map/ppermute | solution.py:130
  12.1 8.6 %collective-permute-start.2 = (bf16[128,512]{1,0:T(8,128)(2,1)S(1)}, bf16[128,512]{1,0:T(8,128)(2,1)S(1)}, u32[]{:S(2)}, u32[]{:S(2)}) collective-permute-start(bf16[128,512]{1,0:T(8,128)(2,1)S(1)} %pad_maximum_fusion.2), channel_id=1, source_target_pairs={{0,3},{1,0},{2,1},{3,2},{4,7},{5,4},{6,5},{7,6},{8,11},{9,8},{10,9... | collective-permute-start | bytes 393224 | tf_op jit(solution)/shard_map/ppermute | solution.py:130
  20.7 0.8 copy-start.2
  21.6 6.1 %copy-start.7 = (s32[4096]{0:T(1024)S(1)}, s32[4096]{0:T(1024)}, u32[]{:S(2)}) copy-start(s32[4096]{0:T(1024)} %doc_ref.7) | copy-start | bytes 49156
  22.8 17.4 %collective-permute-start.3 = (bf16[128,2048]{1,0:T(8,128)(2,1)}, bf16[128,2048]{1,0:T(8,128)(2,1)S(1)}, u32[]{:S(2)}, u32[]{:S(2)}) collective-permute-start(bf16[128,2048]{1,0:T(8,128)(2,1)} %get-tuple-element.10), channel_id=1, source_target_pairs={{0,1},{1,2},{2,3},{3,0},{4,5},{5,6},{6,7},{7,4},{8,9},{9,10},{10,1... | collective-permute-start | bytes 1572872 | tf_op jit(solution)/shard_map/ppermute | solution.py:148
  26.0 61.2 %collective-permute-start.7 = (bf16[128,2048]{1,0:T(8,128)(2,1)S(1)}, bf16[128,2048]{1,0:T(8,128)(2,1)S(1)}, u32[]{:S(2)}, u32[]{:S(2)}) collective-permute-start(bf16[128,2048]{1,0:T(8,128)(2,1)S(1)} %get-tuple-element.9), channel_id=1, source_target_pairs={{0,3},{1,0},{2,1},{3,2},{4,7},{5,4},{6,5},{7,6},{8,11},{9,8},{10,9... | collective-permute-start | bytes 1572872 | tf_op jit(solution)/shard_map/ppermute | solution.py:148
  27.1 47.9 %collective-permute-start.5 = (bf16[128,2048]{1,0:T(8,128)(2,1)S(1)}, bf16[128,2048]{1,0:T(8,128)(2,1)S(1)}, u32[]{:S(2)}, u32[]{:S(2)}) collective-permute-start(bf16[128,2048]{1,0:T(8,128)(2,1)S(1)} %get-tuple-element.12), channel_id=1, source_target_pairs={{0,2},{1,3},{2,0},{3,1},{4,6},{5,7},{6,4},{7,5},{8,10},{9,11},{10,... | collective-permute-start | bytes 1572872 | tf_op jit(solution)/shard_map/ppermute | solution.py:148
  28.8 30.7 %copy-start.11 = (s32[128]{0:T(128)}, s32[128]{0:T(128)S(1)}, u32[]{:S(2)}) copy-start(s32[128]{0:T(128)S(1)} %get-tuple-element.6) | copy-start | bytes 1540
  28.8 41.4 %copy-start.8 = (s32[128]{0:T(128)}, s32[128]{0:T(128)S(1)}, u32[]{:S(2)}) copy-start(s32[128]{0:T(128)S(1)} %get-tuple-element.8) | copy-start | bytes 1540
  28.8 41.4 %copy-start.9 = (s32[128]{0:T(128)}, s32[128]{0:T(128)S(1)}, u32[]{:S(2)}) copy-start(s32[128]{0:T(128)S(1)} %get-tuple-element.5) | copy-start | bytes 1540
  28.8 41.4 %copy-start.10 = (s32[128]{0:T(128)}, s32[128]{0:T(128)S(1)}, u32[]{:S(2)}) copy-start(s32[128]{0:T(128)S(1)} %get-tuple-element.7) | copy-start | bytes 1540
  40.2 19.2 %copy-start.6 = (bf16[128,2048]{1,0:T(8,128)(2,1)}, bf16[128,2048]{1,0:T(8,128)(2,1)S(1)}, u32[]{:S(2)}) copy-start(bf16[128,2048]{1,0:T(8,128)(2,1)S(1)} %collective-permute-done.3.q_ref) | copy-start | bytes 1572868
  70.2 41.5 %collective-permute-start.4 = (bf16[128,2048]{1,0:T(8,128)(2,1)}, bf16[128,2048]{1,0:T(8,128)(2,1)S(1)}, u32[]{:S(2)}, u32[]{:S(2)}) collective-permute-start(bf16[128,2048]{1,0:T(8,128)(2,1)} %shard_map.47), channel_id=1, source_target_pairs={{0,3},{1,0},{2,1},{3,2},{4,7},{5,4},{6,5},{7,6},{8,11},{9,8},{10,9... | collective-permute-start | bytes 1572872 | tf_op jit(solution)/shard_map/ppermute | solution.py:152
  75.0 0.8 copy-start.5
  86.6 36.4 %collective-permute-start.6 = (bf16[128,2048]{1,0:T(8,128)(2,1)}, bf16[128,2048]{1,0:T(8,128)(2,1)S(1)}, u32[]{:S(2)}, u32[]{:S(2)}) collective-permute-start(bf16[128,2048]{1,0:T(8,128)(2,1)} %shard_map.48), channel_id=1, source_target_pairs={{0,2},{1,3},{2,0},{3,1},{4,6},{5,7},{6,4},{7,5},{8,10},{9,11},{10,... | collective-permute-start | bytes 1572872 | tf_op jit(solution)/shard_map/ppermute | solution.py:152
  87.2 0.8 copy-start.4
  98.7 24.3 %collective-permute-start.8 = (bf16[128,2048]{1,0:T(8,128)(2,1)}, bf16[128,2048]{1,0:T(8,128)(2,1)S(1)}, u32[]{:S(2)}, u32[]{:S(2)}) collective-permute-start(bf16[128,2048]{1,0:T(8,128)(2,1)} %shard_map.49), channel_id=1, source_target_pairs={{0,1},{1,2},{2,3},{3,0},{4,5},{5,6},{6,7},{7,4},{8,9},{9,10},{10,1... | collective-permute-start | bytes 1572872 | tf_op jit(solution)/shard_map/ppermute | solution.py:152
  110.6 1.0 copy-start.1
  123.0 1.3 %copy-start = (bf16[128,8192]{1,0:T(8,128)(2,1)}, bf16[128,8192]{1,0:T(8,128)(2,1)S(1)}, u32[]{:S(2)}) copy-start(bf16[128,8192]{1,0:T(8,128)(2,1)S(1)} %constant_dynamic-update-slice_fusion.1) | copy-start | bytes 6291460
Sparse Core Ops, SparseCore 0:
  21.7 37.7 all-gather.1
where the time goes:
time: 135 us; the launch traced here: 132 us
  waiting for transfers between devices  47.5 us (35%)
  Pallas kernels  43 us (32%)
  starting transfers between devices  15.3 us (11%)
  between operations  14.4 us (11%)
  local copies, waits for them, and re-layouts  8.31 us (6%)
  other arithmetic  3.52 us (3%)
    pallas_call x4, Pallas kernels, attend(): pl.pallas_call(kernel, out_shape=jax.ShapeDtypeStruct((q_rows, width), jn...  43 us
    all_gather x1, waiting for transfers between devices, gather_kv(): return lax.all_gather(local, 'seq', axis=0, tiled=True)  19.2 us
    ppermute x3, waiting for transfers between devices, body(): lax.ppermute(out_tile, 'head', [(i, (i - t) % head_count) for i in range(...  11.2 us
    ppermute x3, waiting for transfers between devices, body(): lax.ppermute(piece, 'head', [(i, (i + t) % head_count) for i in range(hea...  10 us
    ppermute x3, waiting for transfers between devices, gather_kv(): lax.ppermute(piece, 'head', [(i, (i + t) % head_count) for i in range(hea...  7.01 us
    ppermute x3, starting transfers between devices, gather_kv(): lax.ppermute(piece, 'head', [(i, (i + t) % head_count) for i in range(hea...  5.68 us
    ppermute x3, starting transfers between devices, body(): lax.ppermute(piece, 'head', [(i, (i + t) % head_count) for i in range(hea...  4.91 us
    ppermute x3, starting transfers between devices, body(): lax.ppermute(out_tile, 'head', [(i, (i - t) % head_count) for i in range(...  4.68 us
  transfers between devices with their start and end apart: 10, of which 5 were waited for; matrix products, arithmetic and copies ran while one was open for 4% of the time, Pallas kernels for 33%

commit v1 on v0

v1 whole, which is shorter than its diff:
```python
import functools
import math

import jax
import jax.numpy as jnp
from jax import lax
from jax.experimental import pallas as pl
from jax.experimental.pallas import tpu as pltpu
from jax.sharding import PartitionSpec as P

HEAD_DIM = 128
KEY_ROWS = 512
DOC_MOST = 3584
NEG_START = -1e30


def flash_kernel(meta_ref, doc_ref, q_ref, ka_ref, va_ref, kb_ref, vb_ref, qstart_ref, o_ref, qt_sc, m_sc, l_sc,
                 acc_sc, *, heads_per, groups, q_rows, steps, scale, sub, head_count):
    step = pl.program_id(0)
    first_block = meta_ref[0]
    last_block = meta_ref[1]
    q_off = meta_ref[2]
    head = meta_ref[3]
    key_block = jnp.minimum(first_block + step, last_block)
    active = first_block + step <= last_block
    full = (key_block * KEY_ROWS + KEY_ROWS - 1 < q_off) & (
        doc_ref[key_block * KEY_ROWS] == doc_ref[q_off + q_rows - 1]
    )

    @pl.when(step == 0)
    def _():
        m_sc[...] = jnp.full(m_sc.shape, NEG_START, jnp.float32)
        l_sc[...] = jnp.zeros(l_sc.shape, jnp.float32)
        acc_sc[...] = jnp.zeros(acc_sc.shape, jnp.float32)
        for j in range(groups * heads_per):
            cols = slice(j * HEAD_DIM, (j + 1) * HEAD_DIM)
            qt_sc[j] = q_ref[:, cols].astype(jnp.float32).T.astype(jnp.bfloat16)

    def compute(masked):
        parts = [(ka_ref, va_ref), (kb_ref, vb_ref)]
        if masked:
            query_pos = q_off + lax.broadcasted_iota(jnp.int32, (sub, q_rows), 1)
            row = lax.broadcasted_iota(jnp.int32, (sub, q_rows), 0)
            visibles = []
            for t in range(head_count):
                key_pos = key_block * KEY_ROWS + ((head - t + head_count) % head_count) * sub + row
                visibles.append((key_pos <= query_pos) & (key_pos >= qstart_ref[...]))
            visibles = [visibles[0], jnp.concatenate(visibles[1:], axis=0)]
        for g in range(groups):
            kcols = slice(g * HEAD_DIM, (g + 1) * HEAD_DIM)
            keys = [k[:, kcols] for k, _ in parts]
            values_t = [v[:, kcols].T for _, v in parts]
            for r in range(heads_per):
                j = g * heads_per + r
                scores = [jnp.dot(k, qt_sc[j], preferred_element_type=jnp.float32) for k in keys]
                if masked:
                    scores = [jnp.where(vis, s, -jnp.inf) for vis, s in zip(visibles, scores)]
                m_old = m_sc[j]
                m_new = jnp.maximum(
                    m_old, jnp.maximum(jnp.max(scores[0], axis=0, keepdims=True), jnp.max(scores[1], axis=0, keepdims=True))
                )
                weights = [jnp.exp2((s - m_new) * scale) for s in scores]
                factor = jnp.exp2((m_old - m_new) * scale)
                l_sc[j] = l_sc[j] * factor + (
                    jnp.sum(weights[0], axis=0, keepdims=True) + jnp.sum(weights[1], axis=0, keepdims=True)
                )
                product = jnp.dot(values_t[0], weights[0].astype(jnp.bfloat16), preferred_element_type=jnp.float32)
                product = product + jnp.dot(
                    values_t[1], weights[1].astype(jnp.bfloat16), preferred_element_type=jnp.float32
                )
                acc_sc[j] = acc_sc[j] * factor + product
                m_sc[j] = m_new

    @pl.when(active & full)
    def _():
        compute(False)

    @pl.when(active & jnp.logical_not(full))
    def _():
        compute(True)

    @pl.when(step == steps - 1)
    def _():
        for j in range(groups * heads_per):
            cols = slice(j * HEAD_DIM, (j + 1) * HEAD_DIM)
            o_ref[:, cols] = (acc_sc[j] / l_sc[j]).T.astype(o_ref.dtype)


def attend(q_tile, q_off, kv_own, kv_rest, doc_ids, groups, heads_per):
    tokens = doc_ids.shape[0]
    q_rows = q_tile.shape[0]
    blocks = tokens // KEY_ROWS
    steps = min(blocks, -(-DOC_MOST // KEY_ROWS) + 1)
    head_count = lax.axis_size("head")
    sub = kv_own.shape[1]
    query_doc = lax.dynamic_slice_in_dim(doc_ids, q_off, q_rows)
    query_start = jnp.sum((doc_ids[None, :] < query_doc[:, None]).astype(jnp.int32), axis=1).reshape(1, q_rows)
    meta = jnp.stack(
        [query_start[0, 0] // KEY_ROWS, (q_off + q_rows - 1) // KEY_ROWS, q_off, lax.axis_index("head")]
    ).astype(jnp.int32)
    width = groups * heads_per * HEAD_DIM
    kv_width = groups * HEAD_DIM
    heads = groups * heads_per
    rest = kv_rest.shape[1]

    def key_index(j, meta, docs):
        return jnp.minimum(meta[0] + j, meta[1])

    kernel = functools.partial(
        flash_kernel, heads_per=heads_per, groups=groups, q_rows=q_rows, steps=steps,
        scale=math.log2(math.e) / HEAD_DIM**0.5, sub=sub, head_count=head_count,
    )
    return pl.pallas_call(
        kernel,
        out_shape=jax.ShapeDtypeStruct((q_rows, width), jnp.bfloat16),
        grid_spec=pltpu.PrefetchScalarGridSpec(
            num_scalar_prefetch=2,
            grid=(steps,),
            in_specs=[
                pl.BlockSpec((q_rows, width), lambda j, meta, docs: (0, 0)),
                pl.BlockSpec((None, sub, kv_width), lambda j, meta, docs: (key_index(j, meta, docs), 0, 0)),
                pl.BlockSpec((None, sub, kv_width), lambda j, meta, docs: (key_index(j, meta, docs), 0, 1)),
                pl.BlockSpec((None, rest, kv_width), lambda j, meta, docs: (key_index(j, meta, docs), 0, 0)),
                pl.BlockSpec((None, rest, kv_width), lambda j, meta, docs: (key_index(j, meta, docs), 0, 1)),
                pl.BlockSpec((1, q_rows), lambda j, meta, docs: (0, 0)),
            ],
            out_specs=pl.BlockSpec((q_rows, width), lambda j, meta, docs: (0, 0)),
            scratch_shapes=[
                pltpu.VMEM((heads, HEAD_DIM, q_rows), jnp.bfloat16),
                pltpu.VMEM((heads, 1, q_rows), jnp.float32),
                pltpu.VMEM((heads, 1, q_rows), jnp.float32),
                pltpu.VMEM((heads, HEAD_DIM, q_rows), jnp.float32),
            ],
        ),
        compiler_params=pltpu.CompilerParams(dimension_semantics=("arbitrary",)),
    )(meta, doc_ids, q_tile, kv_own, kv_own, kv_rest, kv_rest, query_start)


def gather_kv(key_rows, value_rows):
    head_count = lax.axis_size("head")
    head = lax.axis_index("head")
    width = key_rows.shape[1] // head_count
    pieces = []
    for t in range(head_count):
        cols = ((head + t) % head_count) * width
        piece = jnp.concatenate(
            [lax.dynamic_slice_in_dim(key_rows, cols, width, axis=1),
             lax.dynamic_slice_in_dim(value_rows, cols, width, axis=1)], axis=1)
        if t:
            piece = lax.ppermute(piece, "head", [(i, (i + t) % head_count) for i in range(head_count)])
        pieces.append(piece)
    kv_own = lax.all_gather(pieces[0], "seq", axis=0)
    kv_rest = lax.all_gather(jnp.concatenate(pieces[1:], axis=0), "seq", axis=0)
    return kv_own, kv_rest


def body(query_rows, key_rows, value_rows, doc_ids):
    head_count = lax.axis_size("head")
    head = lax.axis_index("head")
    sub = query_rows.shape[0]
    q_width = query_rows.shape[1] // head_count
    groups = key_rows.shape[1] // HEAD_DIM // head_count
    heads_per = query_rows.shape[1] // key_rows.shape[1]
    block_start = lax.axis_index("seq") * sub * head_count
    kv_own, kv_rest = gather_kv(key_rows, value_rows)
    result = jnp.zeros_like(query_rows)
    for t in range(head_count):
        piece = lax.dynamic_slice_in_dim(query_rows, ((head + t) % head_count) * q_width, q_width, axis=1)
        if t:
            piece = lax.ppermute(piece, "head", [(i, (i + t) % head_count) for i in range(head_count)])
        q_off = block_start + ((head - t) % head_count) * sub
        out_tile = attend(piece, q_off, kv_own, kv_rest, doc_ids, groups, heads_per)
        if t:
            out_tile = lax.ppermute(out_tile, "head", [(i, (i - t) % head_count) for i in range(head_count)])
        result = lax.dynamic_update_slice_in_dim(result, out_tile, ((head + t) % head_count) * q_width, axis=1)
    return result


def solution(mesh):
    placed = (P(("seq", "head"), None), P(("seq", "head"), None), P(("seq", "head"), None), P())
    return jax.shard_map(
        body, mesh=mesh, in_specs=placed, out_specs=P(("seq", "head"), None), check_vma=False
    )
```

time: 135 us -> 145 us (1.074); the launches traced: 132 us -> 144 us
  Pallas kernels: 43 us -> 50.5 us
  waiting for transfers between devices: 47.5 us -> 51.2 us
    pallas_call x4, Pallas kernels: 43 us -> 50.5 us  [attend(): pl.pallas_call(kernel, out_shape=jax.ShapeDtypeStruct((q_rows, width), jn...]
    all_gather x1 -> x2, waiting for transfers between devices: 19.2 us -> 26.4 us  [the longest x1 26.4 us: gather_kv(): kv_rest = lax.all_gather(jnp.concatenate(pieces[1:], axis=0), 'seq', axis=0)]
    ppermute x3, waiting for transfers between devices: 11.2 us -> 7.55 us  [body(): lax.ppermute(out_tile, 'head', [(i, (i - t) % head_count) for i in range(...]
    unnamed x24 -> x22, local copies, waits for them, and re-layouts: 4.55 us -> 3.76 us
  transfers between devices with their start and end apart: 10 -> 11, of which waited for: 5 -> 5; matrix products, arithmetic and copies ran while one was open for 4% -> 4% of each run, Pallas kernels for 33% -> 35%
where the time goes in v1:
time: 145 us; the launch traced here: 144 us
  waiting for transfers between devices  51.2 us (35%)
  Pallas kernels  50.5 us (35%)
  starting transfers between devices  15.3 us (11%)
  between operations  14.3 us (10%)
  local copies, waits for them, and re-layouts  7.44 us (5%)
  other arithmetic  4.85 us (3%)
    pallas_call x4, Pallas kernels, attend(): pl.pallas_call(kernel, out_shape=jax.ShapeDtypeStruct((q_rows, width), jn...  50.5 us
    all_gather x1, waiting for transfers between devices, gather_kv(): kv_rest = lax.all_gather(jnp.concatenate(pieces[1:], axis=0), 'seq', axis=0)  26.4 us
    ppermute x3, waiting for transfers between devices, body(): lax.ppermute(piece, 'head', [(i, (i + t) % head_count) for i in range(hea...  10.1 us
    ppermute x3, waiting for transfers between devices, body(): lax.ppermute(out_tile, 'head', [(i, (i - t) % head_count) for i in range(...  7.55 us
    ppermute x3, waiting for transfers between devices, gather_kv(): lax.ppermute(piece, 'head', [(i, (i + t) % head_count) for i in range(hea...  7.15 us
    ppermute x3, starting transfers between devices, gather_kv(): lax.ppermute(piece, 'head', [(i, (i + t) % head_count) for i in range(hea...  5.68 us
    ppermute x3, starting transfers between devices, body(): lax.ppermute(piece, 'head', [(i, (i + t) % head_count) for i in range(hea...  4.91 us
    ppermute x3, starting transfers between devices, body(): lax.ppermute(out_tile, 'head', [(i, (i - t) % head_count) for i in range(...  4.67 us
  transfers between devices with their start and end apart: 11, of which 5 were waited for; matrix products, arithmetic and copies ran while one was open for 4% of the time, Pallas kernels for 35%

profile of v1, /device:TPU:6, one launch (start us, length us, event | category | flops | bytes accessed | tf_op | source)
XLA Modules:
  0.0 143.6 jit_solution(14278558270329952774)
XLA Ops:
  6.5 1.3 constant_dynamic-slice_fusion.7
  7.8 0.7 pad_maximum_fusion.1
  8.5 0.0 all-gather.5.cloned.1.call-update
  8.5 0.0 all-gather.7.cloned.1.call-start
  8.5 1.6 %collective-permute-start = (bf16[128,512]{1,0:T(8,128)(2,1)S(1)}, bf16[128,512]{1,0:T(8,128)(2,1)S(1)}, u32[]{:S(2)}, u32[]{:S(2)}) collective-permute-start(bf16[128,512]{1,0:T(8,128)(2,1)S(1)} %pad_maximum_fusion.2), channel_id=1, source_target_pairs={{0,1},{1,2},{2,3},{3,0},{4,5},{5,6},{6,7},{7,4},{8,9},{9,10},{10,1... | collective-permute-start | bytes 393224 | tf_op jit(solution)/shard_map/ppermute | solution.py:150
  10.2 2.7 %collective-permute-start.1 = (bf16[128,512]{1,0:T(8,128)(2,1)S(1)}, bf16[128,512]{1,0:T(8,128)(2,1)S(1)}, u32[]{:S(2)}, u32[]{:S(2)}) collective-permute-start(bf16[128,512]{1,0:T(8,128)(2,1)S(1)} %pad_maximum_fusion.3), channel_id=1, source_target_pairs={{0,2},{1,3},{2,0},{3,1},{4,6},{5,7},{6,4},{7,5},{8,10},{9,11},{10,... | collective-permute-start | bytes 393224 | tf_op jit(solution)/shard_map/ppermute | solution.py:150
  12.9 1.4 collective-permute-start.2
  14.3 2.6 %collective-permute-done = bf16[128,512]{1,0:T(8,128)(2,1)S(1)} collective-permute-done((bf16[128,512]{1,0:T(8,128)(2,1)S(1)}, bf16[128,512]{1,0:T(8,128)(2,1)S(1)}, u32[]{:S(2)}, u32[]{:S(2)}) %collective-permute-start) | collective-permute-done | bytes 131104 | tf_op jit(solution)/shard_map/ppermute | solution.py:150
  16.9 4.5 %collective-permute-done.1 = bf16[128,512]{1,0:T(8,128)(2,1)S(1)} collective-permute-done((bf16[128,512]{1,0:T(8,128)(2,1)S(1)}, bf16[128,512]{1,0:T(8,128)(2,1)S(1)}, u32[]{:S(2)}, u32[]{:S(2)}) %collective-permute-start.1) | collective-permute-done | bytes 131104 | tf_op jit(solution)/shard_map/ppermute | solution.py:150
  21.4 0.0 collective-permute-done.2
  21.4 0.8 pad_maximum_fusion
  22.2 0.0 all-gather.7.cloned.1.call-update
  22.3 0.0 copy-start.6
  22.3 1.2 constant_dynamic-slice_fusion
  23.4 3.3 %collective-permute-start.3 = (bf16[128,2048]{1,0:T(8,128)(2,1)}, bf16[128,2048]{1,0:T(8,128)(2,1)S(1)}, u32[]{:S(2)}, u32[]{:S(2)}) collective-permute-start(bf16[128,2048]{1,0:T(8,128)(2,1)} %get-tuple-element.10), channel_id=1, source_target_pairs={{0,1},{1,2},{2,3},{3,0},{4,5},{5,6},{6,7},{7,4},{8,9},{9,10},{10,1... | collective-permute-start | bytes 1572872 | tf_op jit(solution)/shard_map/ppermute | solution.py:170
  26.7 1.1 collective-permute-start.7
  27.8 0.6 collective-permute-start.5
  28.4 0.1 fusion
  28.4 1.0 convert_reduce_fusion
  29.4 0.0 copy-start.7
  29.5 0.0 copy-start.8
  29.5 0.0 copy-start.9
  30.2 0.6 add_add_fusion.1.meta_ref
  30.8 10.1 %collective-permute-done.3.q_ref = bf16[128,2048]{1,0:T(8,128)(2,1)S(1)} collective-permute-done((bf16[128,2048]{1,0:T(8,128)(2,1)}, bf16[128,2048]{1,0:T(8,128)(2,1)S(1)}, u32[]{:S(2)}, u32[]{:S(2)}) %collective-permute-start.3) | collective-permute-done | bytes 524320 | tf_op jit(solution)/shard_map/ppermute | solution.py:170
  40.9 26.4 %all-gather.7.cloned.1.call-done = bf16[3072,512]{1,0:T(8,128)(2,1)} async-done(((bf16[384,512]{1,0:T(8,128)(2,1)}), bf16[3072,512]{1,0:T(8,128)(2,1)}) %all-gather.7.cloned.1.call-update) | async-done | bytes 3145744 | tf_op jit(solution)/shard_map/all_gather | solution.py:153
  67.3 12.6 %shard_map.47 = bf16[128,2048]{1,0:T(8,128)(2,1)} custom-call(s32[4]{0:T(128)} %add_add_fusion.1.meta_ref, s32[4096]{0:T(1024)} %doc_ref.7, bf16[128,2048]{1,0:T(8,128)(2,1)} %copy-done.5, bf16[8,128,512]{2,1,0:T(8,128)(2,1)} %bitcast.35, bf16[8,128,512]{2,1,0:T(8,128)(2,1)} %bitcast.36, bf16[8,384,512]{2,1,0:T(8,128)(2,1)} %bitcast.27, ...), custom_call_target="tpu_custom_call" | custom-call | tf_op jit(solution)/shard_map/pallas_call | solution.py:113
  79.9 0.0 copy-done.9
  79.9 3.6 %collective-permute-start.4 = (bf16[128,2048]{1,0:T(8,128)(2,1)}, bf16[128,2048]{1,0:T(8,128)(2,1)S(1)}, u32[]{:S(2)}, u32[]{:S(2)}) collective-permute-start(bf16[128,2048]{1,0:T(8,128)(2,1)} %shard_map.47), channel_id=1, source_target_pairs={{0,3},{1,0},{2,1},{3,2},{4,7},{5,4},{6,5},{7,6},{8,11},{9,8},{10,9... | collective-permute-start | bytes 1572872 | tf_op jit(solution)/shard_map/ppermute | solution.py:174
  83.5 0.6 add_add_fusion.3.meta_ref
  84.1 0.6 add_add_fusion.2.meta_ref
  84.7 0.0 collective-permute-done.5.q_ref
  84.7 0.8 copy-done.4
  85.5 12.6 %shard_map.48 = bf16[128,2048]{1,0:T(8,128)(2,1)} custom-call(s32[4]{0:T(128)} %add_add_fusion.2.meta_ref, s32[4096]{0:T(1024)} %doc_ref.7, bf16[128,2048]{1,0:T(8,128)(2,1)} %copy-done.4, bf16[8,128,512]{2,1,0:T(8,128)(2,1)} %bitcast.37, bf16[8,128,512]{2,1,0:T(8,128)(2,1)} %bitcast.38, bf16[8,384,512]{2,1,0:T(8,128)(2,1)} %bitcast.29, ...), custom_call_target="tpu_custom_call" | custom-call | tf_op jit(solution)/shard_map/pallas_call | solution.py:113
  98.1 0.0 collective-permute-start.6
  98.1 0.6 add_add_fusion.meta_ref
  98.7 0.0 collective-permute-done.7.q_ref
  98.7 0.8 copy-done.3
  99.5 12.6 %shard_map.49 = bf16[128,2048]{1,0:T(8,128)(2,1)} custom-call(s32[4]{0:T(128)} %add_add_fusion.3.meta_ref, s32[4096]{0:T(1024)} %doc_ref.7, bf16[128,2048]{1,0:T(8,128)(2,1)} %copy-done.3, bf16[8,128,512]{2,1,0:T(8,128)(2,1)} %bitcast.39, bf16[8,128,512]{2,1,0:T(8,128)(2,1)} %bitcast.40, bf16[8,384,512]{2,1,0:T(8,128)(2,1)} %bitcast.31, ...), custom_call_target="tpu_custom_call" | custom-call | tf_op jit(solution)/shard_map/pallas_call | solution.py:113
  112.1 1.1 collective-permute-start.8
  113.2 12.6 %shard_map.46 = bf16[128,2048]{1,0:T(8,128)(2,1)} custom-call(s32[4]{0:T(128)} %add_add_fusion.meta_ref, s32[4096]{0:T(1024)} %doc_ref.7, bf16[128,2048]{1,0:T(8,128)(2,1)} %get-tuple-element.11.q_ref, bf16[8,128,512]{2,1,0:T(8,128)(2,1)} %bitcast.41, bf16[8,128,512]{2,1,0:T(8,128)(2,1)} %bitcast.42, bf16[8,384,512]{2,1,0:T(8,128)(2,1)} %bitcast.33, ...), custom_call_target="tpu_custom_call" | custom-call | tf_op jit(solution)/shard_map/pallas_call | solution.py:113
  125.8 0.2 broadcast_in_dim.2
  126.0 0.8 copy-done.1
  126.9 0.0 collective-permute-done.4
  127.0 7.5 %collective-permute-done.6 = bf16[128,2048]{1,0:T(8,128)(2,1)S(1)} collective-permute-done((bf16[128,2048]{1,0:T(8,128)(2,1)}, bf16[128,2048]{1,0:T(8,128)(2,1)S(1)}, u32[]{:S(2)}, u32[]{:S(2)}) %collective-permute-start.6) | collective-permute-done | bytes 524320 | tf_op jit(solution)/shard_map/ppermute | solution.py:174
  134.6 0.0 copy-start
  134.6 0.0 collective-permute-done.8
  134.6 1.3 copy-done
  135.9 0.8 constant_dynamic-update-slice_fusion
  (20 shorter events, 0.2 us)
Async XLA Ops:
  6.5 15.7 %copy-start.2 = (bf16[128,8192]{1,0:T(8,128)(2,1)S(1)}, bf16[128,8192]{1,0:T(8,128)(2,1)}, u32[]{:S(2)}) copy-start(bf16[128,8192]{1,0:T(8,128)(2,1)} %param.4) | copy-start | bytes 6291460
  6.5 34.4 %all-gather.5.cloned.1.call-start = ((), (), s32[]{:S(2)}) async-start(), calls=%async_computation | async-start | bytes 1179648 | tf_op jit(solution)/shard_map/all_gather | solution.py:152
  8.5 58.8 %all-gather.7.cloned.1.call-start = ((), (), s32[]{:S(2)}) async-start(), calls=%async_computation.1 | async-start | bytes 3538944 | tf_op jit(solution)/shard_map/all_gather | solution.py:153
  8.5 8.3 %collective-permute-start = (bf16[128,512]{1,0:T(8,128)(2,1)S(1)}, bf16[128,512]{1,0:T(8,128)(2,1)S(1)}, u32[]{:S(2)}, u32[]{:S(2)}) collective-permute-start(bf16[128,512]{1,0:T(8,128)(2,1)S(1)} %pad_maximum_fusion.2), channel_id=1, source_target_pairs={{0,1},{1,2},{2,3},{3,0},{4,5},{5,6},{6,7},{7,4},{8,9},{9,10},{10,1... | collective-permute-start | bytes 393224 | tf_op jit(solution)/shard_map/ppermute | solution.py:150
  10.2 11.2 %collective-permute-start.1 = (bf16[128,512]{1,0:T(8,128)(2,1)S(1)}, bf16[128,512]{1,0:T(8,128)(2,1)S(1)}, u32[]{:S(2)}, u32[]{:S(2)}) collective-permute-start(bf16[128,512]{1,0:T(8,128)(2,1)S(1)} %pad_maximum_fusion.3), channel_id=1, source_target_pairs={{0,2},{1,3},{2,0},{3,1},{4,6},{5,7},{6,4},{7,5},{8,10},{9,11},{10,... | collective-permute-start | bytes 393224 | tf_op jit(solution)/shard_map/ppermute | solution.py:150
  12.9 8.6 %collective-permute-start.2 = (bf16[128,512]{1,0:T(8,128)(2,1)S(1)}, bf16[128,512]{1,0:T(8,128)(2,1)S(1)}, u32[]{:S(2)}, u32[]{:S(2)}) collective-permute-start(bf16[128,512]{1,0:T(8,128)(2,1)S(1)} %pad_maximum_fusion.4), channel_id=1, source_target_pairs={{0,3},{1,0},{2,1},{3,2},{4,7},{5,4},{6,5},{7,6},{8,11},{9,8},{10,9... | collective-permute-start | bytes 393224 | tf_op jit(solution)/shard_map/ppermute | solution.py:150
  22.3 6.1 %copy-start.6 = (s32[4096]{0:T(1024)S(1)}, s32[4096]{0:T(1024)}, u32[]{:S(2)}) copy-start(s32[4096]{0:T(1024)} %doc_ref.7) | copy-start | bytes 49156
  23.4 17.4 %collective-permute-start.3 = (bf16[128,2048]{1,0:T(8,128)(2,1)}, bf16[128,2048]{1,0:T(8,128)(2,1)S(1)}, u32[]{:S(2)}, u32[]{:S(2)}) collective-permute-start(bf16[128,2048]{1,0:T(8,128)(2,1)} %get-tuple-element.10), channel_id=1, source_target_pairs={{0,1},{1,2},{2,3},{3,0},{4,5},{5,6},{6,7},{7,4},{8,9},{9,10},{10,1... | collective-permute-start | bytes 1572872 | tf_op jit(solution)/shard_map/ppermute | solution.py:170
  26.7 72.0 %collective-permute-start.7 = (bf16[128,2048]{1,0:T(8,128)(2,1)S(1)}, bf16[128,2048]{1,0:T(8,128)(2,1)S(1)}, u32[]{:S(2)}, u32[]{:S(2)}) collective-permute-start(bf16[128,2048]{1,0:T(8,128)(2,1)S(1)} %get-tuple-element.9), channel_id=1, source_target_pairs={{0,3},{1,0},{2,1},{3,2},{4,7},{5,4},{6,5},{7,6},{8,11},{9,8},{10,9... | collective-permute-start | bytes 1572872 | tf_op jit(solution)/shard_map/ppermute | solution.py:170
  27.8 56.9 %collective-permute-start.5 = (bf16[128,2048]{1,0:T(8,128)(2,1)S(1)}, bf16[128,2048]{1,0:T(8,128)(2,1)S(1)}, u32[]{:S(2)}, u32[]{:S(2)}) collective-permute-start(bf16[128,2048]{1,0:T(8,128)(2,1)S(1)} %get-tuple-element.12), channel_id=1, source_target_pairs={{0,2},{1,3},{2,0},{3,1},{4,6},{5,7},{6,4},{7,5},{8,10},{9,11},{10,... | collective-permute-start | bytes 1572872 | tf_op jit(solution)/shard_map/ppermute | solution.py:170
  29.4 37.8 %copy-start.10 = (s32[128]{0:T(128)}, s32[128]{0:T(128)S(1)}, u32[]{:S(2)}) copy-start(s32[128]{0:T(128)S(1)} %get-tuple-element.6) | copy-start | bytes 1540
  29.4 50.4 %copy-start.7 = (s32[128]{0:T(128)}, s32[128]{0:T(128)S(1)}, u32[]{:S(2)}) copy-start(s32[128]{0:T(128)S(1)} %get-tuple-element.8) | copy-start | bytes 1540
  29.5 50.4 %copy-start.8 = (s32[128]{0:T(128)}, s32[128]{0:T(128)S(1)}, u32[]{:S(2)}) copy-start(s32[128]{0:T(128)S(1)} %get-tuple-element.5) | copy-start | bytes 1540
  29.5 50.4 %copy-start.9 = (s32[128]{0:T(128)}, s32[128]{0:T(128)S(1)}, u32[]{:S(2)}) copy-start(s32[128]{0:T(128)S(1)} %get-tuple-element.7) | copy-start | bytes 1540
  40.9 26.4 %copy-start.5 = (bf16[128,2048]{1,0:T(8,128)(2,1)}, bf16[128,2048]{1,0:T(8,128)(2,1)S(1)}, u32[]{:S(2)}) copy-start(bf16[128,2048]{1,0:T(8,128)(2,1)S(1)} %collective-permute-done.3.q_ref) | copy-start | bytes 1572868
  79.9 47.0 %collective-permute-start.4 = (bf16[128,2048]{1,0:T(8,128)(2,1)}, bf16[128,2048]{1,0:T(8,128)(2,1)S(1)}, u32[]{:S(2)}, u32[]{:S(2)}) collective-permute-start(bf16[128,2048]{1,0:T(8,128)(2,1)} %shard_map.47), channel_id=1, source_target_pairs={{0,3},{1,0},{2,1},{3,2},{4,7},{5,4},{6,5},{7,6},{8,11},{9,8},{10,9... | collective-permute-start | bytes 1572872 | tf_op jit(solution)/shard_map/ppermute | solution.py:174
  84.7 0.8 copy-start.4
  98.1 36.4 %collective-permute-start.6 = (bf16[128,2048]{1,0:T(8,128)(2,1)}, bf16[128,2048]{1,0:T(8,128)(2,1)S(1)}, u32[]{:S(2)}, u32[]{:S(2)}) collective-permute-start(bf16[128,2048]{1,0:T(8,128)(2,1)} %shard_map.48), channel_id=1, source_target_pairs={{0,2},{1,3},{2,0},{3,1},{4,6},{5,7},{6,4},{7,5},{8,10},{9,11},{10,... | collective-permute-start | bytes 1572872 | tf_op jit(solution)/shard_map/ppermute | solution.py:174
  98.7 0.8 copy-start.3
  112.1 22.5 %collective-permute-start.8 = (bf16[128,2048]{1,0:T(8,128)(2,1)}, bf16[128,2048]{1,0:T(8,128)(2,1)S(1)}, u32[]{:S(2)}, u32[]{:S(2)}) collective-permute-start(bf16[128,2048]{1,0:T(8,128)(2,1)} %shard_map.49), channel_id=1, source_target_pairs={{0,1},{1,2},{2,3},{3,0},{4,5},{5,6},{6,7},{7,4},{8,9},{9,10},{10,1... | collective-permute-start | bytes 1572872 | tf_op jit(solution)/shard_map/ppermute | solution.py:174
  125.8 1.0 copy-start.1
  134.6 1.3 copy-start
Sparse Core Ops, SparseCore 0:
  9.2 23.7 all-gather.4
  34.9 32.2 all-gather.6

commit v2 on v0

--- a/solution.py
+++ b/solution.py
@@ -14,7 +14,7 @@
 NEG_START = -1e30
 
 
-def flash_kernel(meta_ref, doc_ref, q_ref, k_ref, v_ref, qstart_ref, o_ref, qt_sc, m_sc, l_sc, acc_sc,
+def flash_kernel(meta_ref, doc_ref, qt_ref, k_ref, v_ref, qstart_ref, o_ref, m_sc, l_sc, acc_sc,
                  *, heads_per, groups, q_rows, steps, scale):
     step = pl.program_id(0)
     first_block = meta_ref[0]
@@ -31,9 +31,6 @@
         m_sc[...] = jnp.full(m_sc.shape, NEG_START, jnp.float32)
         l_sc[...] = jnp.zeros(l_sc.shape, jnp.float32)
         acc_sc[...] = jnp.zeros(acc_sc.shape, jnp.float32)
-        for j in range(groups * heads_per):
-            cols = slice(j * HEAD_DIM, (j + 1) * HEAD_DIM)
-            qt_sc[j] = q_ref[:, cols].astype(jnp.float32).T.astype(jnp.bfloat16)
 
     def compute(masked):
         if masked:
@@ -45,7 +42,7 @@
             values_t = v_ref[:, g * HEAD_DIM:(g + 1) * HEAD_DIM].T
             for r in range(heads_per):
                 j = g * heads_per + r
-                scores = jnp.dot(keys, qt_sc[j], preferred_element_type=jnp.float32)
+                scores = jnp.dot(keys, qt_ref[j], preferred_element_type=jnp.float32)
                 if masked:
                     scores = jnp.where(visible, scores, -jnp.inf)
                 m_old = m_sc[j]
@@ -74,7 +71,7 @@
 
 def attend(q_tile, q_off, kv_rows, doc_ids, groups, heads_per):
     tokens = doc_ids.shape[0]
-    q_rows = q_tile.shape[0]
+    q_rows = q_tile.shape[2]
     blocks = tokens // KEY_ROWS
     steps = min(blocks, -(-DOC_MOST // KEY_ROWS) + 1)
     query_doc = lax.dynamic_slice_in_dim(doc_ids, q_off, q_rows)
@@ -98,14 +95,13 @@
             num_scalar_prefetch=2,
             grid=(steps,),
             in_specs=[
-                pl.BlockSpec((q_rows, width), lambda j, meta, docs: (0, 0)),
+                pl.BlockSpec((groups * heads_per, HEAD_DIM, q_rows), lambda j, meta, docs: (0, 0, 0)),
                 pl.BlockSpec((KEY_ROWS, kv_width), lambda j, meta, docs: (key_index(j, meta, docs), 0)),
                 pl.BlockSpec((KEY_ROWS, kv_width), lambda j, meta, docs: (key_index(j, meta, docs), 1)),
                 pl.BlockSpec((1, q_rows), lambda j, meta, docs: (0, 0)),
             ],
             out_specs=pl.BlockSpec((q_rows, width), lambda j, meta, docs: (0, 0)),
             scratch_shapes=[
-                pltpu.VMEM((heads, HEAD_DIM, q_rows), jnp.bfloat16),
                 pltpu.VMEM((heads, 1, q_rows), jnp.float32),
                 pltpu.VMEM((heads, 1, q_rows), jnp.float32),
                 pltpu.VMEM((heads, HEAD_DIM, q_rows), jnp.float32),
@@ -144,6 +140,7 @@
     result = jnp.zeros_like(query_rows)
     for t in range(head_count):
         piece = lax.dynamic_slice_in_dim(query_rows, ((head + t) % head_count) * q_width, q_width, axis=1)
+        piece = piece.reshape(sub, q_width // HEAD_DIM, HEAD_DIM).transpose(1, 2, 0)
         if t:
             piece = lax.ppermute(piece, "head", [(i, (i + t) % head_count) for i in range(head_count)])
         q_off = block_start + ((head - t) % head_count) * sub

time: 135 us -> 143 us (1.059); the launches traced: 132 us -> 144 us
  starting transfers between devices: 15.3 us -> 33.7 us
  waiting for transfers between devices: 47.5 us -> 36.6 us
  local copies, waits for them, and re-layouts: 8.31 us -> 13.7 us
    ppermute x3, starting transfers between devices: 4.68 us -> 23 us  [body(): lax.ppermute(out_tile, 'head', [(i, (i - t) % head_count) for i in range(...]
    ppermute x3, waiting for transfers between devices: 11.2 us -> 0.06 us  [body(): lax.ppermute(out_tile, 'head', [(i, (i - t) % head_count) for i in range(...]
    dynamic_slice x1 -> x5, local copies, waits for them, and re-layouts: 1.18 us -> 6.59 us  [body(): lax.dynamic_slice_in_dim(query_rows, (head + t) % head_count * q_width, q...]
    ppermute x3, waiting for transfers between devices: 10 us -> 12.4 us  [body(): lax.ppermute(piece, 'head', [(i, (i + t) % head_count) for i in range(hea...]
    all_gather x1, waiting for transfers between devices: 19.2 us -> 17.1 us  [gather_kv(): return lax.all_gather(local, 'seq', axis=0, tiled=True)]
  transfers between devices with their start and end apart: 10 -> 10, of which waited for: 5 -> 6; matrix products, arithmetic and copies ran while one was open for 4% -> 7% of each run, Pallas kernels for 33% -> 29%
where the time goes in v2:
time: 143 us; the launch traced here: 144 us
  Pallas kernels  42.6 us (30%)
  waiting for transfers between devices  36.6 us (26%)
  starting transfers between devices  33.7 us (24%)
  between operations  14.4 us (10%)
  local copies, waits for them, and re-layouts  13.7 us (10%)
  other arithmetic  3.53 us (2%)
    pallas_call x4, Pallas kernels, attend(): pl.pallas_call(kernel, out_shape=jax.ShapeDtypeStruct((q_rows, width), jn...  42.6 us
    ppermute x3, starting transfers between devices, body(): lax.ppermute(out_tile, 'head', [(i, (i - t) % head_count) for i in range(...  23 us
    all_gather x1, waiting for transfers between devices, gather_kv(): return lax.all_gather(local, 'seq', axis=0, tiled=True)  17.1 us
    ppermute x3, waiting for transfers between devices, body(): lax.ppermute(piece, 'head', [(i, (i + t) % head_count) for i in range(hea...  12.4 us
    ppermute x3, waiting for transfers between devices, gather_kv(): lax.ppermute(piece, 'head', [(i, (i + t) % head_count) for i in range(hea...  7.01 us
    dynamic_slice x5, local copies, waits for them, and re-layouts, body(): lax.dynamic_slice_in_dim(query_rows, (head + t) % head_count * q_width, q...  6.59 us
    ppermute x3, starting transfers between devices, gather_kv(): lax.ppermute(piece, 'head', [(i, (i + t) % head_count) for i in range(hea...  5.68 us
    ppermute x3, starting transfers between devices, body(): lax.ppermute(piece, 'head', [(i, (i + t) % head_count) for i in range(hea...  4.97 us
  transfers between devices with their start and end apart: 10, of which 6 were waited for; matrix products, arithmetic and copies ran while one was open for 7% of the time, Pallas kernels for 29%

profile of v2, /device:TPU:6, one launch (start us, length us, event | category | flops | bytes accessed | tf_op | source)
XLA Modules:
  0.0 144.5 jit_solution(8139900863858303554)
XLA Ops:
  6.5 0.0 all-gather.2.cloned.1.call-start
  6.5 1.3 constant_dynamic-slice_fusion.3
  7.8 1.6 %collective-permute-start = (bf16[128,512]{1,0:T(8,128)(2,1)S(1)}, bf16[128,512]{1,0:T(8,128)(2,1)S(1)}, u32[]{:S(2)}, u32[]{:S(2)}) collective-permute-start(bf16[128,512]{1,0:T(8,128)(2,1)S(1)} %pad_maximum_fusion), channel_id=1, source_target_pairs={{0,1},{1,2},{2,3},{3,0},{4,5},{5,6},{6,7},{7,4},{8,9},{9,10},{10,1... | collective-permute-start | bytes 393224 | tf_op jit(solution)/shard_map/ppermute | solution.py:126
  9.5 2.7 %collective-permute-start.1 = (bf16[128,512]{1,0:T(8,128)(2,1)S(1)}, bf16[128,512]{1,0:T(8,128)(2,1)S(1)}, u32[]{:S(2)}, u32[]{:S(2)}) collective-permute-start(bf16[128,512]{1,0:T(8,128)(2,1)S(1)} %pad_maximum_fusion.1), channel_id=1, source_target_pairs={{0,2},{1,3},{2,0},{3,1},{4,6},{5,7},{6,4},{7,5},{8,10},{9,11},{10,... | collective-permute-start | bytes 393224 | tf_op jit(solution)/shard_map/ppermute | solution.py:126
  12.1 1.4 collective-permute-start.2
  13.7 2.5 %collective-permute-done = bf16[128,512]{1,0:T(8,128)(2,1)S(1)} collective-permute-done((bf16[128,512]{1,0:T(8,128)(2,1)S(1)}, bf16[128,512]{1,0:T(8,128)(2,1)S(1)}, u32[]{:S(2)}, u32[]{:S(2)}) %collective-permute-start) | collective-permute-done | bytes 131104 | tf_op jit(solution)/shard_map/ppermute | solution.py:126
  16.2 4.5 %collective-permute-done.1 = bf16[128,512]{1,0:T(8,128)(2,1)S(1)} collective-permute-done((bf16[128,512]{1,0:T(8,128)(2,1)S(1)}, bf16[128,512]{1,0:T(8,128)(2,1)S(1)}, u32[]{:S(2)}, u32[]{:S(2)}) %collective-permute-start.1) | collective-permute-done | bytes 131104 | tf_op jit(solution)/shard_map/ppermute | solution.py:126
  20.7 0.0 collective-permute-done.2
  20.7 0.0 copy-start.2
  20.7 0.8 copy-done.2
  21.5 0.0 all-gather.2.cloned.1.call-update
  21.6 1.2 constant_dynamic-slice_fusion
  22.8 2.1 %copy.10 = bf16[128,2048]{0,1:T(8,128)(2,1)} copy(bf16[128,2048]{1,0:T(8,128)(2,1)} %get-tuple-element.10) | data formatting | bytes 1048576 | tf_op jit(solution)/shard_map/dynamic_slice | solution.py:142
  24.9 3.2 %collective-permute-start.3 = (bf16[16,128,128]{2,1,0:T(8,128)(2,1)}, bf16[16,128,128]{2,1,0:T(8,128)(2,1)S(1)}, u32[]{:S(2)}, u32[]{:S(2)}) collective-permute-start(bf16[16,128,128]{2,1,0:T(8,128)(2,1)} %bitcast.13), channel_id=1, source_target_pairs={{0,1},{1,2},{2,3},{3,0},{4,5},{5,6},{6,7},{7,4},{8,9},{9,10},{10,1... | collective-permute-start | bytes 1572872 | tf_op jit(solution)/shard_map/ppermute | solution.py:145
  28.1 1.3 copy.12
  29.4 1.2 collective-permute-start.7
  30.6 1.0 copy.11
  31.6 0.6 collective-permute-start.5
  32.2 0.0 copy-done.7
  32.2 0.1 fusion
  32.3 1.0 convert_reduce_fusion
  34.0 0.6 pad_add_fusion.1.meta_ref
  34.6 7.7 %collective-permute-done.3.qt_ref = bf16[16,128,128]{2,1,0:T(8,128)(2,1)S(1)} collective-permute-done((bf16[16,128,128]{2,1,0:T(8,128)(2,1)}, bf16[16,128,128]{2,1,0:T(8,128)(2,1)S(1)}, u32[]{:S(2)}, u32[]{:S(2)}) %collective-permute-start.3) | collective-permute-done | bytes 524320 | tf_op jit(solution)/shard_map/ppermute | solution.py:145
  42.3 17.1 %all-gather.2.cloned.1.call-done.k_ref.v_ref = bf16[4096,512]{1,0:T(8,128)(2,1)} async-done(((bf16[512,512]{1,0:T(8,128)(2,1)}), bf16[4096,512]{1,0:T(8,128)(2,1)}) %all-gather.2.cloned.1.call-update) | async-done | bytes 4194320 | tf_op jit(solution)/shard_map/all_gather | solution.py:128
  59.4 5.5 %shard_map.47 = bf16[128,2048]{1,0:T(8,128)(2,1)} custom-call(s32[3]{0:T(128)} %pad_add_fusion.1.meta_ref, s32[4096]{0:T(1024)} %doc_ref.7, bf16[16,128,128]{2,1,0:T(8,128)(2,1)} %copy-done.6, bf16[4096,512]{1,0:T(8,128)(2,1)} %all-gather.2.cloned.1.call-done.k_ref.v_ref, bf16[4096,512]{1,0:T(8,128)(2,1)} %all-gather.2.cloned.1.call-done.k_ref.v_ref, ...), custom_call_target="tpu_custom_call" | custom-call | tf_op jit(solution)/shard_map/pallas_call | solution.py:91
  64.9 0.0 copy-done.8
  64.9 3.6 %collective-permute-start.4 = (bf16[128,2048]{1,0:T(8,128)(2,1)}, bf16[128,2048]{1,0:T(8,128)(2,1)S(1)}, u32[]{:S(2)}, u32[]{:S(2)}) collective-permute-start(bf16[128,2048]{1,0:T(8,128)(2,1)} %shard_map.47), channel_id=1, source_target_pairs={{0,3},{1,0},{2,1},{3,2},{4,7},{5,4},{6,5},{7,6},{8,11},{9,8},{10,9... | collective-permute-start | bytes 1572872 | tf_op jit(solution)/shard_map/ppermute | solution.py:149
  68.5 0.6 pad_add_fusion.3.meta_ref
  69.1 0.7 pad_add_fusion.2.meta_ref
  69.8 4.7 %collective-permute-done.5.qt_ref = bf16[16,128,128]{2,1,0:T(8,128)(2,1)S(1)} collective-permute-done((bf16[16,128,128]{2,1,0:T(8,128)(2,1)}, bf16[16,128,128]{2,1,0:T(8,128)(2,1)S(1)}, u32[]{:S(2)}, u32[]{:S(2)}) %collective-permute-start.5) | collective-permute-done | bytes 524320 | tf_op jit(solution)/shard_map/ppermute | solution.py:145
  74.5 0.8 copy-done.5
  75.3 5.5 %shard_map.48 = bf16[128,2048]{1,0:T(8,128)(2,1)} custom-call(s32[3]{0:T(128)} %pad_add_fusion.2.meta_ref, s32[4096]{0:T(1024)} %doc_ref.7, bf16[16,128,128]{2,1,0:T(8,128)(2,1)} %copy-done.5, bf16[4096,512]{1,0:T(8,128)(2,1)} %all-gather.2.cloned.1.call-done.k_ref.v_ref, bf16[4096,512]{1,0:T(8,128)(2,1)} %all-gather.2.cloned.1.call-done.k_ref.v_ref, ...), custom_call_target="tpu_custom_call" | custom-call | tf_op jit(solution)/shard_map/pallas_call | solution.py:91
  80.8 15.0 %collective-permute-start.6 = (bf16[128,2048]{1,0:T(8,128)(2,1)}, bf16[128,2048]{1,0:T(8,128)(2,1)S(1)}, u32[]{:S(2)}, u32[]{:S(2)}) collective-permute-start(bf16[128,2048]{1,0:T(8,128)(2,1)} %shard_map.48), channel_id=1, source_target_pairs={{0,2},{1,3},{2,0},{3,1},{4,6},{5,7},{6,4},{7,5},{8,10},{9,11},{10,... | collective-permute-start | bytes 1572872 | tf_op jit(solution)/shard_map/ppermute | solution.py:149
  95.8 0.6 pad_add_fusion.meta_ref
  96.4 1.0 copy.9
  97.4 0.0 collective-permute-done.7.qt_ref
  97.4 0.8 copy-done.4
  98.2 16.3 %shard_map.49 = bf16[128,2048]{1,0:T(8,128)(2,1)} custom-call(s32[3]{0:T(128)} %pad_add_fusion.3.meta_ref, s32[4096]{0:T(1024)} %doc_ref.7, bf16[16,128,128]{2,1,0:T(8,128)(2,1)} %copy-done.4, bf16[4096,512]{1,0:T(8,128)(2,1)} %all-gather.2.cloned.1.call-done.k_ref.v_ref, bf16[4096,512]{1,0:T(8,128)(2,1)} %all-gather.2.cloned.1.call-done.k_ref.v_ref, ...), custom_call_target="tpu_custom_call" | custom-call | tf_op jit(solution)/shard_map/pallas_call | solution.py:91
  114.4 4.4 %collective-permute-start.8 = (bf16[128,2048]{1,0:T(8,128)(2,1)}, bf16[128,2048]{1,0:T(8,128)(2,1)S(1)}, u32[]{:S(2)}, u32[]{:S(2)}) collective-permute-start(bf16[128,2048]{1,0:T(8,128)(2,1)} %shard_map.49), channel_id=1, source_target_pairs={{0,1},{1,2},{2,3},{3,0},{4,5},{5,6},{6,7},{7,4},{8,9},{9,10},{10,1... | collective-permute-start | bytes 1572872 | tf_op jit(solution)/shard_map/ppermute | solution.py:149
  118.9 15.4 %shard_map.46 = bf16[128,2048]{1,0:T(8,128)(2,1)} custom-call(s32[3]{0:T(128)} %pad_add_fusion.meta_ref, s32[4096]{0:T(1024)} %doc_ref.7, bf16[16,128,128]{2,1,0:T(8,128)(2,1)} %bitcast.36, bf16[4096,512]{1,0:T(8,128)(2,1)} %all-gather.2.cloned.1.call-done.k_ref.v_ref, bf16[4096,512]{1,0:T(8,128)(2,1)} %all-gather.2.cloned.1.call-done.k_ref.v_ref, ...), custom_call_target="tpu_custom_call" | custom-call | tf_op jit(solution)/shard_map/pallas_call | solution.py:91
  134.2 0.2 broadcast_in_dim.4
  134.4 0.8 copy-done.1
  135.3 0.0 collective-permute-done.4
  135.4 0.0 collective-permute-done.6
  135.5 0.0 copy-start
  135.5 0.1 collective-permute-done.8
  135.5 1.3 copy-done
  136.8 0.8 constant_dynamic-update-slice_fusion
  (26 shorter events, 0.3 us)
Async XLA Ops:
  6.5 52.9 %all-gather.2.cloned.1.call-start = ((), (), s32[]{:S(2)}) async-start(), calls=%async_computation | async-start | bytes 4718592 | tf_op jit(solution)/shard_map/all_gather | solution.py:128
  6.5 15.1 %copy-start.3 = (bf16[128,8192]{1,0:T(8,128)(2,1)S(1)}, bf16[128,8192]{1,0:T(8,128)(2,1)}, u32[]{:S(2)}) copy-start(bf16[128,8192]{1,0:T(8,128)(2,1)} %param.4) | copy-start | bytes 6291460
  7.8 8.3 %collective-permute-start = (bf16[128,512]{1,0:T(8,128)(2,1)S(1)}, bf16[128,512]{1,0:T(8,128)(2,1)S(1)}, u32[]{:S(2)}, u32[]{:S(2)}) collective-permute-start(bf16[128,512]{1,0:T(8,128)(2,1)S(1)} %pad_maximum_fusion), channel_id=1, source_target_pairs={{0,1},{1,2},{2,3},{3,0},{4,5},{5,6},{6,7},{7,4},{8,9},{9,10},{10,1... | collective-permute-start | bytes 393224 | tf_op jit(solution)/shard_map/ppermute | solution.py:126
  9.5 11.2 %collective-permute-start.1 = (bf16[128,512]{1,0:T(8,128)(2,1)S(1)}, bf16[128,512]{1,0:T(8,128)(2,1)S(1)}, u32[]{:S(2)}, u32[]{:S(2)}) collective-permute-start(bf16[128,512]{1,0:T(8,128)(2,1)S(1)} %pad_maximum_fusion.1), channel_id=1, source_target_pairs={{0,2},{1,3},{2,0},{3,1},{4,6},{5,7},{6,4},{7,5},{8,10},{9,11},{10,... | collective-permute-start | bytes 393224 | tf_op jit(solution)/shard_map/ppermute | solution.py:126
  12.1 8.6 %collective-permute-start.2 = (bf16[128,512]{1,0:T(8,128)(2,1)S(1)}, bf16[128,512]{1,0:T(8,128)(2,1)S(1)}, u32[]{:S(2)}, u32[]{:S(2)}) collective-permute-start(bf16[128,512]{1,0:T(8,128)(2,1)S(1)} %pad_maximum_fusion.2), channel_id=1, source_target_pairs={{0,3},{1,0},{2,1},{3,2},{4,7},{5,4},{6,5},{7,6},{8,11},{9,8},{10,9... | collective-permute-start | bytes 393224 | tf_op jit(solution)/shard_map/ppermute | solution.py:126
  20.7 0.8 copy-start.2
  22.8 9.4 %copy-start.7 = (s32[4096]{0:T(1024)S(1)}, s32[4096]{0:T(1024)}, u32[]{:S(2)}) copy-start(s32[4096]{0:T(1024)} %doc_ref.7) | copy-start | bytes 49156
  24.9 17.4 %collective-permute-start.3 = (bf16[16,128,128]{2,1,0:T(8,128)(2,1)}, bf16[16,128,128]{2,1,0:T(8,128)(2,1)S(1)}, u32[]{:S(2)}, u32[]{:S(2)}) collective-permute-start(bf16[16,128,128]{2,1,0:T(8,128)(2,1)} %bitcast.13), channel_id=1, source_target_pairs={{0,1},{1,2},{2,3},{3,0},{4,5},{5,6},{6,7},{7,4},{8,9},{9,10},{10,1... | collective-permute-start | bytes 1572872 | tf_op jit(solution)/shard_map/ppermute | solution.py:145
  29.4 67.9 %collective-permute-start.7 = (bf16[16,128,128]{2,1,0:T(8,128)(2,1)S(1)}, bf16[16,128,128]{2,1,0:T(8,128)(2,1)S(1)}, u32[]{:S(2)}, u32[]{:S(2)}) collective-permute-start(bf16[16,128,128]{2,1,0:T(8,128)(2,1)S(1)} %bitcast.37), channel_id=1, source_target_pairs={{0,3},{1,0},{2,1},{3,2},{4,7},{5,4},{6,5},{7,6},{8,11},{9,8},{10,9... | collective-permute-start | bytes 1572872 | tf_op jit(solution)/shard_map/ppermute | solution.py:145
  31.6 42.9 %collective-permute-start.5 = (bf16[16,128,128]{2,1,0:T(8,128)(2,1)}, bf16[16,128,128]{2,1,0:T(8,128)(2,1)S(1)}, u32[]{:S(2)}, u32[]{:S(2)}) collective-permute-start(bf16[16,128,128]{2,1,0:T(8,128)(2,1)} %bitcast.38), channel_id=1, source_target_pairs={{0,2},{1,3},{2,0},{3,1},{4,6},{5,7},{6,4},{7,5},{8,10},{9,11},{10,... | collective-permute-start | bytes 1572872 | tf_op jit(solution)/shard_map/ppermute | solution.py:145
  33.2 26.2 %copy-start.11 = (s32[128]{0:T(128)}, s32[128]{0:T(128)S(1)}, u32[]{:S(2)}) copy-start(s32[128]{0:T(128)S(1)} %get-tuple-element.6) | copy-start | bytes 1540
  33.3 31.7 %copy-start.8 = (s32[128]{0:T(128)}, s32[128]{0:T(128)S(1)}, u32[]{:S(2)}) copy-start(s32[128]{0:T(128)S(1)} %get-tuple-element.8) | copy-start | bytes 1540
  33.3 31.7 %copy-start.9 = (s32[128]{0:T(128)}, s32[128]{0:T(128)S(1)}, u32[]{:S(2)}) copy-start(s32[128]{0:T(128)S(1)} %get-tuple-element.5) | copy-start | bytes 1540
  33.3 31.7 %copy-start.10 = (s32[128]{0:T(128)}, s32[128]{0:T(128)S(1)}, u32[]{:S(2)}) copy-start(s32[128]{0:T(128)S(1)} %get-tuple-element.7) | copy-start | bytes 1540
  42.3 17.1 %copy-start.6 = (bf16[16,128,128]{2,1,0:T(8,128)(2,1)}, bf16[16,128,128]{2,1,0:T(8,128)(2,1)S(1)}, u32[]{:S(2)}) copy-start(bf16[16,128,128]{2,1,0:T(8,128)(2,1)S(1)} %collective-permute-done.3.qt_ref) | copy-start | bytes 1572868
  64.9 70.4 %collective-permute-start.4 = (bf16[128,2048]{1,0:T(8,128)(2,1)}, bf16[128,2048]{1,0:T(8,128)(2,1)S(1)}, u32[]{:S(2)}, u32[]{:S(2)}) collective-permute-start(bf16[128,2048]{1,0:T(8,128)(2,1)} %shard_map.47), channel_id=1, source_target_pairs={{0,3},{1,0},{2,1},{3,2},{4,7},{5,4},{6,5},{7,6},{8,11},{9,8},{10,9... | collective-permute-start | bytes 1572872 | tf_op jit(solution)/shard_map/ppermute | solution.py:149
  74.5 0.8 copy-start.5
  80.8 54.6 %collective-permute-start.6 = (bf16[128,2048]{1,0:T(8,128)(2,1)}, bf16[128,2048]{1,0:T(8,128)(2,1)S(1)}, u32[]{:S(2)}, u32[]{:S(2)}) collective-permute-start(bf16[128,2048]{1,0:T(8,128)(2,1)} %shard_map.48), channel_id=1, source_target_pairs={{0,2},{1,3},{2,0},{3,1},{4,6},{5,7},{6,4},{7,5},{8,10},{9,11},{10,... | collective-permute-start | bytes 1572872 | tf_op jit(solution)/shard_map/ppermute | solution.py:149
  97.4 0.8 copy-start.4
  114.4 21.1 %collective-permute-start.8 = (bf16[128,2048]{1,0:T(8,128)(2,1)}, bf16[128,2048]{1,0:T(8,128)(2,1)S(1)}, u32[]{:S(2)}, u32[]{:S(2)}) collective-permute-start(bf16[128,2048]{1,0:T(8,128)(2,1)} %shard_map.49), channel_id=1, source_target_pairs={{0,1},{1,2},{2,3},{3,0},{4,5},{5,6},{6,7},{7,4},{8,9},{9,10},{10,1... | collective-permute-start | bytes 1572872 | tf_op jit(solution)/shard_map/ppermute | solution.py:149
  134.2 1.0 copy-start.1
  135.5 1.3 copy-start
Sparse Core Ops, SparseCore 0:
  21.7 37.7 all-gather.1

commit v3 on v0

--- a/solution.py
+++ b/solution.py
@@ -33,7 +33,7 @@
         acc_sc[...] = jnp.zeros(acc_sc.shape, jnp.float32)
         for j in range(groups * heads_per):
             cols = slice(j * HEAD_DIM, (j + 1) * HEAD_DIM)
-            qt_sc[j] = q_ref[:, cols].astype(jnp.float32).T.astype(jnp.bfloat16)
+            qt_sc[j] = q_ref[:, cols].T
 
     def compute(masked):
         if masked:

time: 135 us -> 134 us (level)
  no operation moved by 1% of the time
where the time goes in v3:
time: 134 us; the launch traced here: 132 us
  waiting for transfers between devices  47.6 us (36%)
  Pallas kernels  43 us (32%)
  starting transfers between devices  15.3 us (11%)
  between operations  14.4 us (11%)
  local copies, waits for them, and re-layouts  8.31 us (6%)
  other arithmetic  3.52 us (3%)
    pallas_call x4, Pallas kernels, attend(): pl.pallas_call(kernel, out_shape=jax.ShapeDtypeStruct((q_rows, width), jn...  43 us
    all_gather x1, waiting for transfers between devices, gather_kv(): return lax.all_gather(local, 'seq', axis=0, tiled=True)  19.2 us
    ppermute x3, waiting for transfers between devices, body(): lax.ppermute(out_tile, 'head', [(i, (i - t) % head_count) for i in range(...  11.3 us
    ppermute x3, waiting for transfers between devices, body(): lax.ppermute(piece, 'head', [(i, (i + t) % head_count) for i in range(hea...  10 us
    ppermute x3, waiting for transfers between devices, gather_kv(): lax.ppermute(piece, 'head', [(i, (i + t) % head_count) for i in range(hea...  7.01 us
    ppermute x3, starting transfers between devices, gather_kv(): lax.ppermute(piece, 'head', [(i, (i + t) % head_count) for i in range(hea...  5.68 us
    ppermute x3, starting transfers between devices, body(): lax.ppermute(piece, 'head', [(i, (i + t) % head_count) for i in range(hea...  4.91 us
    ppermute x3, starting transfers between devices, body(): lax.ppermute(out_tile, 'head', [(i, (i - t) % head_count) for i in range(...  4.67 us
  transfers between devices with their start and end apart: 10, of which 5 were waited for; matrix products, arithmetic and copies ran while one was open for 4% of the time, Pallas kernels for 33%

profile of v3, /device:TPU:6, one launch (start us, length us, event | category | flops | bytes accessed | tf_op | source)
XLA Modules:
  0.0 132.0 jit_solution(15208560604672204334)
XLA Ops:
  6.5 0.0 all-gather.2.cloned.1.call-start
  6.5 1.3 constant_dynamic-slice_fusion.3
  7.8 1.6 %collective-permute-start = (bf16[128,512]{1,0:T(8,128)(2,1)S(1)}, bf16[128,512]{1,0:T(8,128)(2,1)S(1)}, u32[]{:S(2)}, u32[]{:S(2)}) collective-permute-start(bf16[128,512]{1,0:T(8,128)(2,1)S(1)} %pad_maximum_fusion), channel_id=1, source_target_pairs={{0,1},{1,2},{2,3},{3,0},{4,5},{5,6},{6,7},{7,4},{8,9},{9,10},{10,1... | collective-permute-start | bytes 393224 | tf_op jit(solution)/shard_map/ppermute | solution.py:130
  9.5 2.7 %collective-permute-start.1 = (bf16[128,512]{1,0:T(8,128)(2,1)S(1)}, bf16[128,512]{1,0:T(8,128)(2,1)S(1)}, u32[]{:S(2)}, u32[]{:S(2)}) collective-permute-start(bf16[128,512]{1,0:T(8,128)(2,1)S(1)} %pad_maximum_fusion.1), channel_id=1, source_target_pairs={{0,2},{1,3},{2,0},{3,1},{4,6},{5,7},{6,4},{7,5},{8,10},{9,11},{10,... | collective-permute-start | bytes 393224 | tf_op jit(solution)/shard_map/ppermute | solution.py:130
  12.1 1.4 %collective-permute-start.2 = (bf16[128,512]{1,0:T(8,128)(2,1)S(1)}, bf16[128,512]{1,0:T(8,128)(2,1)S(1)}, u32[]{:S(2)}, u32[]{:S(2)}) collective-permute-start(bf16[128,512]{1,0:T(8,128)(2,1)S(1)} %pad_maximum_fusion.2), channel_id=1, source_target_pairs={{0,3},{1,0},{2,1},{3,2},{4,7},{5,4},{6,5},{7,6},{8,11},{9,8},{10,9... | collective-permute-start | bytes 393224 | tf_op jit(solution)/shard_map/ppermute | solution.py:130
  13.7 2.5 %collective-permute-done = bf16[128,512]{1,0:T(8,128)(2,1)S(1)} collective-permute-done((bf16[128,512]{1,0:T(8,128)(2,1)S(1)}, bf16[128,512]{1,0:T(8,128)(2,1)S(1)}, u32[]{:S(2)}, u32[]{:S(2)}) %collective-permute-start) | collective-permute-done | bytes 131104 | tf_op jit(solution)/shard_map/ppermute | solution.py:130
  16.2 4.5 %collective-permute-done.1 = bf16[128,512]{1,0:T(8,128)(2,1)S(1)} collective-permute-done((bf16[128,512]{1,0:T(8,128)(2,1)S(1)}, bf16[128,512]{1,0:T(8,128)(2,1)S(1)}, u32[]{:S(2)}, u32[]{:S(2)}) %collective-permute-start.1) | collective-permute-done | bytes 131104 | tf_op jit(solution)/shard_map/ppermute | solution.py:130
  20.7 0.0 collective-permute-done.2
  20.7 0.0 copy-start.2
  20.7 0.8 copy-done.2
  21.5 0.0 all-gather.2.cloned.1.call-update
  21.6 0.0 copy-done.3
  21.6 0.0 copy-start.7
  21.6 1.2 constant_dynamic-slice_fusion
  22.8 3.2 %collective-permute-start.3 = (bf16[128,2048]{1,0:T(8,128)(2,1)}, bf16[128,2048]{1,0:T(8,128)(2,1)S(1)}, u32[]{:S(2)}, u32[]{:S(2)}) collective-permute-start(bf16[128,2048]{1,0:T(8,128)(2,1)} %get-tuple-element.10), channel_id=1, source_target_pairs={{0,1},{1,2},{2,3},{3,0},{4,5},{5,6},{6,7},{7,4},{8,9},{9,10},{10,1... | collective-permute-start | bytes 1572872 | tf_op jit(solution)/shard_map/ppermute | solution.py:148
  26.0 1.1 collective-permute-start.7
  27.1 0.6 collective-permute-start.5
  27.7 0.0 copy-done.7
  27.7 0.1 fusion
  27.8 1.0 convert_reduce_fusion
  28.8 0.0 copy-start.8
  28.8 0.0 copy-start.9
  29.5 0.7 pad_add_fusion.1.meta_ref
  30.2 10.0 %collective-permute-done.3.q_ref = bf16[128,2048]{1,0:T(8,128)(2,1)S(1)} collective-permute-done((bf16[128,2048]{1,0:T(8,128)(2,1)}, bf16[128,2048]{1,0:T(8,128)(2,1)S(1)}, u32[]{:S(2)}, u32[]{:S(2)}) %collective-permute-start.3) | collective-permute-done | bytes 524320 | tf_op jit(solution)/shard_map/ppermute | solution.py:148
  40.2 19.2 %all-gather.2.cloned.1.call-done.k_ref.v_ref = bf16[4096,512]{1,0:T(8,128)(2,1)} async-done(((bf16[512,512]{1,0:T(8,128)(2,1)}), bf16[4096,512]{1,0:T(8,128)(2,1)}) %all-gather.2.cloned.1.call-update) | async-done | bytes 4194320 | tf_op jit(solution)/shard_map/all_gather | solution.py:132
  59.5 10.7 %shard_map.47 = bf16[128,2048]{1,0:T(8,128)(2,1)} custom-call(s32[3]{0:T(128)} %pad_add_fusion.1.meta_ref, s32[4096]{0:T(1024)} %doc_ref.7, bf16[128,2048]{1,0:T(8,128)(2,1)} %copy-done.6, bf16[4096,512]{1,0:T(8,128)(2,1)} %all-gather.2.cloned.1.call-done.k_ref.v_ref, bf16[4096,512]{1,0:T(8,128)(2,1)} %all-gather.2.cloned.1.call-done.k_ref.v_ref, ...), custom_call_target="tpu_custom_call" | custom-call | tf_op jit(solution)/shard_map/pallas_call | solution.py:94
  70.2 0.0 copy-done.10
  70.2 3.6 %collective-permute-start.4 = (bf16[128,2048]{1,0:T(8,128)(2,1)}, bf16[128,2048]{1,0:T(8,128)(2,1)S(1)}, u32[]{:S(2)}, u32[]{:S(2)}) collective-permute-start(bf16[128,2048]{1,0:T(8,128)(2,1)} %shard_map.47), channel_id=1, source_target_pairs={{0,3},{1,0},{2,1},{3,2},{4,7},{5,4},{6,5},{7,6},{8,11},{9,8},{10,9... | collective-permute-start | bytes 1572872 | tf_op jit(solution)/shard_map/ppermute | solution.py:152
  73.8 0.6 pad_add_fusion.3.meta_ref
  74.4 0.6 pad_add_fusion.2.meta_ref
  75.0 0.0 collective-permute-done.5.q_ref
  75.0 0.8 copy-done.5
  75.8 10.8 %shard_map.48 = bf16[128,2048]{1,0:T(8,128)(2,1)} custom-call(s32[3]{0:T(128)} %pad_add_fusion.2.meta_ref, s32[4096]{0:T(1024)} %doc_ref.7, bf16[128,2048]{1,0:T(8,128)(2,1)} %copy-done.5, bf16[4096,512]{1,0:T(8,128)(2,1)} %all-gather.2.cloned.1.call-done.k_ref.v_ref, bf16[4096,512]{1,0:T(8,128)(2,1)} %all-gather.2.cloned.1.call-done.k_ref.v_ref, ...), custom_call_target="tpu_custom_call" | custom-call | tf_op jit(solution)/shard_map/pallas_call | solution.py:94
  86.5 0.0 collective-permute-start.6
  86.6 0.6 pad_add_fusion.meta_ref
  87.2 0.0 collective-permute-done.7.q_ref
  87.2 0.8 copy-done.4
  88.0 10.7 %shard_map.49 = bf16[128,2048]{1,0:T(8,128)(2,1)} custom-call(s32[3]{0:T(128)} %pad_add_fusion.3.meta_ref, s32[4096]{0:T(1024)} %doc_ref.7, bf16[128,2048]{1,0:T(8,128)(2,1)} %copy-done.4, bf16[4096,512]{1,0:T(8,128)(2,1)} %all-gather.2.cloned.1.call-done.k_ref.v_ref, bf16[4096,512]{1,0:T(8,128)(2,1)} %all-gather.2.cloned.1.call-done.k_ref.v_ref, ...), custom_call_target="tpu_custom_call" | custom-call | tf_op jit(solution)/shard_map/pallas_call | solution.py:94
  98.7 1.1 collective-permute-start.8
  99.8 10.7 %shard_map.46 = bf16[128,2048]{1,0:T(8,128)(2,1)} custom-call(s32[3]{0:T(128)} %pad_add_fusion.meta_ref, s32[4096]{0:T(1024)} %doc_ref.7, bf16[128,2048]{1,0:T(8,128)(2,1)} %get-tuple-element.11.q_ref, bf16[4096,512]{1,0:T(8,128)(2,1)} %all-gather.2.cloned.1.call-done.k_ref.v_ref, bf16[4096,512]{1,0:T(8,128)(2,1)} %all-gather.2.cloned.1.call-done.k_ref.v_ref, ...), custom_call_target="tpu_custom_call" | custom-call | tf_op jit(solution)/shard_map/pallas_call | solution.py:94
  110.5 0.2 broadcast_in_dim.4
  110.7 0.8 copy-done.1
  111.6 0.0 collective-permute-done.4
  111.7 11.3 %collective-permute-done.6 = bf16[128,2048]{1,0:T(8,128)(2,1)S(1)} collective-permute-done((bf16[128,2048]{1,0:T(8,128)(2,1)}, bf16[128,2048]{1,0:T(8,128)(2,1)S(1)}, u32[]{:S(2)}, u32[]{:S(2)}) %collective-permute-start.6) | collective-permute-done | bytes 524320 | tf_op jit(solution)/shard_map/ppermute | solution.py:152
  123.0 0.0 copy-start
  123.0 0.0 collective-permute-done.8
  123.0 1.3 copy-done
  124.3 0.8 constant_dynamic-update-slice_fusion
  (22 shorter events, 0.3 us)
Async XLA Ops:
  6.5 52.9 %all-gather.2.cloned.1.call-start = ((), (), s32[]{:S(2)}) async-start(), calls=%async_computation | async-start | bytes 4718592 | tf_op jit(solution)/shard_map/all_gather | solution.py:132
  6.5 15.1 %copy-start.3 = (bf16[128,8192]{1,0:T(8,128)(2,1)S(1)}, bf16[128,8192]{1,0:T(8,128)(2,1)}, u32[]{:S(2)}) copy-start(bf16[128,8192]{1,0:T(8,128)(2,1)} %param.4) | copy-start | bytes 6291460
  7.8 8.3 %collective-permute-start = (bf16[128,512]{1,0:T(8,128)(2,1)S(1)}, bf16[128,512]{1,0:T(8,128)(2,1)S(1)}, u32[]{:S(2)}, u32[]{:S(2)}) collective-permute-start(bf16[128,512]{1,0:T(8,128)(2,1)S(1)} %pad_maximum_fusion), channel_id=1, source_target_pairs={{0,1},{1,2},{2,3},{3,0},{4,5},{5,6},{6,7},{7,4},{8,9},{9,10},{10,1... | collective-permute-start | bytes 393224 | tf_op jit(solution)/shard_map/ppermute | solution.py:130
  9.5 11.2 %collective-permute-start.1 = (bf16[128,512]{1,0:T(8,128)(2,1)S(1)}, bf16[128,512]{1,0:T(8,128)(2,1)S(1)}, u32[]{:S(2)}, u32[]{:S(2)}) collective-permute-start(bf16[128,512]{1,0:T(8,128)(2,1)S(1)} %pad_maximum_fusion.1), channel_id=1, source_target_pairs={{0,2},{1,3},{2,0},{3,1},{4,6},{5,7},{6,4},{7,5},{8,10},{9,11},{10,... | collective-permute-start | bytes 393224 | tf_op jit(solution)/shard_map/ppermute | solution.py:130
  12.1 8.6 %collective-permute-start.2 = (bf16[128,512]{1,0:T(8,128)(2,1)S(1)}, bf16[128,512]{1,0:T(8,128)(2,1)S(1)}, u32[]{:S(2)}, u32[]{:S(2)}) collective-permute-start(bf16[128,512]{1,0:T(8,128)(2,1)S(1)} %pad_maximum_fusion.2), channel_id=1, source_target_pairs={{0,3},{1,0},{2,1},{3,2},{4,7},{5,4},{6,5},{7,6},{8,11},{9,8},{10,9... | collective-permute-start | bytes 393224 | tf_op jit(solution)/shard_map/ppermute | solution.py:130
  20.7 0.8 copy-start.2
  21.6 6.1 %copy-start.7 = (s32[4096]{0:T(1024)S(1)}, s32[4096]{0:T(1024)}, u32[]{:S(2)}) copy-start(s32[4096]{0:T(1024)} %doc_ref.7) | copy-start | bytes 49156
  22.8 17.4 %collective-permute-start.3 = (bf16[128,2048]{1,0:T(8,128)(2,1)}, bf16[128,2048]{1,0:T(8,128)(2,1)S(1)}, u32[]{:S(2)}, u32[]{:S(2)}) collective-permute-start(bf16[128,2048]{1,0:T(8,128)(2,1)} %get-tuple-element.10), channel_id=1, source_target_pairs={{0,1},{1,2},{2,3},{3,0},{4,5},{5,6},{6,7},{7,4},{8,9},{9,10},{10,1... | collective-permute-start | bytes 1572872 | tf_op jit(solution)/shard_map/ppermute | solution.py:148
  26.0 61.1 %collective-permute-start.7 = (bf16[128,2048]{1,0:T(8,128)(2,1)S(1)}, bf16[128,2048]{1,0:T(8,128)(2,1)S(1)}, u32[]{:S(2)}, u32[]{:S(2)}) collective-permute-start(bf16[128,2048]{1,0:T(8,128)(2,1)S(1)} %get-tuple-element.9), channel_id=1, source_target_pairs={{0,3},{1,0},{2,1},{3,2},{4,7},{5,4},{6,5},{7,6},{8,11},{9,8},{10,9... | collective-permute-start | bytes 1572872 | tf_op jit(solution)/shard_map/ppermute | solution.py:148
  27.1 47.9 %collective-permute-start.5 = (bf16[128,2048]{1,0:T(8,128)(2,1)S(1)}, bf16[128,2048]{1,0:T(8,128)(2,1)S(1)}, u32[]{:S(2)}, u32[]{:S(2)}) collective-permute-start(bf16[128,2048]{1,0:T(8,128)(2,1)S(1)} %get-tuple-element.12), channel_id=1, source_target_pairs={{0,2},{1,3},{2,0},{3,1},{4,6},{5,7},{6,4},{7,5},{8,10},{9,11},{10,... | collective-permute-start | bytes 1572872 | tf_op jit(solution)/shard_map/ppermute | solution.py:148
  28.8 30.7 %copy-start.11 = (s32[128]{0:T(128)}, s32[128]{0:T(128)S(1)}, u32[]{:S(2)}) copy-start(s32[128]{0:T(128)S(1)} %get-tuple-element.6) | copy-start | bytes 1540
  28.8 41.4 %copy-start.8 = (s32[128]{0:T(128)}, s32[128]{0:T(128)S(1)}, u32[]{:S(2)}) copy-start(s32[128]{0:T(128)S(1)} %get-tuple-element.8) | copy-start | bytes 1540
  28.8 41.4 %copy-start.9 = (s32[128]{0:T(128)}, s32[128]{0:T(128)S(1)}, u32[]{:S(2)}) copy-start(s32[128]{0:T(128)S(1)} %get-tuple-element.5) | copy-start | bytes 1540
  28.8 41.4 %copy-start.10 = (s32[128]{0:T(128)}, s32[128]{0:T(128)S(1)}, u32[]{:S(2)}) copy-start(s32[128]{0:T(128)S(1)} %get-tuple-element.7) | copy-start | bytes 1540
  40.2 19.2 %copy-start.6 = (bf16[128,2048]{1,0:T(8,128)(2,1)}, bf16[128,2048]{1,0:T(8,128)(2,1)S(1)}, u32[]{:S(2)}) copy-start(bf16[128,2048]{1,0:T(8,128)(2,1)S(1)} %collective-permute-done.3.q_ref) | copy-start | bytes 1572868
  70.2 41.4 %collective-permute-start.4 = (bf16[128,2048]{1,0:T(8,128)(2,1)}, bf16[128,2048]{1,0:T(8,128)(2,1)S(1)}, u32[]{:S(2)}, u32[]{:S(2)}) collective-permute-start(bf16[128,2048]{1,0:T(8,128)(2,1)} %shard_map.47), channel_id=1, source_target_pairs={{0,3},{1,0},{2,1},{3,2},{4,7},{5,4},{6,5},{7,6},{8,11},{9,8},{10,9... | collective-permute-start | bytes 1572872 | tf_op jit(solution)/shard_map/ppermute | solution.py:152
  75.0 0.8 copy-start.5
  86.5 36.4 %collective-permute-start.6 = (bf16[128,2048]{1,0:T(8,128)(2,1)}, bf16[128,2048]{1,0:T(8,128)(2,1)S(1)}, u32[]{:S(2)}, u32[]{:S(2)}) collective-permute-start(bf16[128,2048]{1,0:T(8,128)(2,1)} %shard_map.48), channel_id=1, source_target_pairs={{0,2},{1,3},{2,0},{3,1},{4,6},{5,7},{6,4},{7,5},{8,10},{9,11},{10,... | collective-permute-start | bytes 1572872 | tf_op jit(solution)/shard_map/ppermute | solution.py:152
  87.2 0.8 copy-start.4
  98.7 24.3 %collective-permute-start.8 = (bf16[128,2048]{1,0:T(8,128)(2,1)}, bf16[128,2048]{1,0:T(8,128)(2,1)S(1)}, u32[]{:S(2)}, u32[]{:S(2)}) collective-permute-start(bf16[128,2048]{1,0:T(8,128)(2,1)} %shard_map.49), channel_id=1, source_target_pairs={{0,1},{1,2},{2,3},{3,0},{4,5},{5,6},{6,7},{7,4},{8,9},{9,10},{10,1... | collective-permute-start | bytes 1572872 | tf_op jit(solution)/shard_map/ppermute | solution.py:152
  110.5 1.0 copy-start.1
  123.0 1.3 %copy-start = (bf16[128,8192]{1,0:T(8,128)(2,1)}, bf16[128,8192]{1,0:T(8,128)(2,1)S(1)}, u32[]{:S(2)}) copy-start(bf16[128,8192]{1,0:T(8,128)(2,1)S(1)} %constant_dynamic-update-slice_fusion.1) | copy-start | bytes 6291460
Sparse Core Ops, SparseCore 0:
  21.7 37.7 all-gather.1

commit v4 on v0

--- a/solution.py
+++ b/solution.py
@@ -9,7 +9,7 @@
 from jax.sharding import PartitionSpec as P
 
 HEAD_DIM = 128
-KEY_ROWS = 512
+KEY_ROWS = 1024
 DOC_MOST = 3584
 NEG_START = -1e30
 

time: 135 us -> 138 us (1.022); the launches traced: 132 us -> 139 us
  Pallas kernels: 43 us -> 58.5 us
  waiting for transfers between devices: 47.5 us -> 38.6 us
    pallas_call x4, Pallas kernels: 43 us -> 58.5 us  [attend(): pl.pallas_call(kernel, out_shape=jax.ShapeDtypeStruct((q_rows, width), jn...]
    ppermute x3, waiting for transfers between devices: 11.2 us -> 2.37 us  [body(): lax.ppermute(out_tile, 'head', [(i, (i - t) % head_count) for i in range(...]
  transfers between devices with their start and end apart: 10 -> 10, of which waited for: 5 -> 5; matrix products, arithmetic and copies ran while one was open for 4% -> 4% of each run, Pallas kernels for 33% -> 42%
where the time goes in v4:
time: 138 us; the launch traced here: 139 us
  Pallas kernels  58.5 us (42%)
  waiting for transfers between devices  38.6 us (28%)
  starting transfers between devices  15.3 us (11%)
  between operations  14.4 us (10%)
  local copies, waits for them, and re-layouts  8.31 us (6%)
  other arithmetic  3.52 us (3%)
    pallas_call x4, Pallas kernels, attend(): pl.pallas_call(kernel, out_shape=jax.ShapeDtypeStruct((q_rows, width), jn...  58.5 us
    all_gather x1, waiting for transfers between devices, gather_kv(): return lax.all_gather(local, 'seq', axis=0, tiled=True)  19.2 us
    ppermute x3, waiting for transfers between devices, body(): lax.ppermute(piece, 'head', [(i, (i + t) % head_count) for i in range(hea...  10 us
    ppermute x3, waiting for transfers between devices, gather_kv(): lax.ppermute(piece, 'head', [(i, (i + t) % head_count) for i in range(hea...  7.01 us
    ppermute x3, starting transfers between devices, gather_kv(): lax.ppermute(piece, 'head', [(i, (i + t) % head_count) for i in range(hea...  5.68 us
    ppermute x3, starting transfers between devices, body(): lax.ppermute(piece, 'head', [(i, (i + t) % head_count) for i in range(hea...  4.91 us
    ppermute x3, starting transfers between devices, body(): lax.ppermute(out_tile, 'head', [(i, (i - t) % head_count) for i in range(...  4.67 us
    unnamed x24, local copies, waits for them, and re-layouts  4.55 us
  transfers between devices with their start and end apart: 10, of which 5 were waited for; matrix products, arithmetic and copies ran while one was open for 4% of the time, Pallas kernels for 42%

profile of v4, /device:TPU:6, one launch (start us, length us, event | category | flops | bytes accessed | tf_op | source)
XLA Modules:
  0.0 138.6 jit_solution(11510507714991753055)
XLA Ops:
  6.5 0.0 all-gather.2.cloned.1.call-start
  6.5 1.3 constant_dynamic-slice_fusion.3
  7.8 1.6 %collective-permute-start = (bf16[128,512]{1,0:T(8,128)(2,1)S(1)}, bf16[128,512]{1,0:T(8,128)(2,1)S(1)}, u32[]{:S(2)}, u32[]{:S(2)}) collective-permute-start(bf16[128,512]{1,0:T(8,128)(2,1)S(1)} %pad_maximum_fusion), channel_id=1, source_target_pairs={{0,1},{1,2},{2,3},{3,0},{4,5},{5,6},{6,7},{7,4},{8,9},{9,10},{10,1... | collective-permute-start | bytes 393224 | tf_op jit(solution)/shard_map/ppermute | solution.py:130
  9.5 2.7 %collective-permute-start.1 = (bf16[128,512]{1,0:T(8,128)(2,1)S(1)}, bf16[128,512]{1,0:T(8,128)(2,1)S(1)}, u32[]{:S(2)}, u32[]{:S(2)}) collective-permute-start(bf16[128,512]{1,0:T(8,128)(2,1)S(1)} %pad_maximum_fusion.1), channel_id=1, source_target_pairs={{0,2},{1,3},{2,0},{3,1},{4,6},{5,7},{6,4},{7,5},{8,10},{9,11},{10,... | collective-permute-start | bytes 393224 | tf_op jit(solution)/shard_map/ppermute | solution.py:130
  12.1 1.4 %collective-permute-start.2 = (bf16[128,512]{1,0:T(8,128)(2,1)S(1)}, bf16[128,512]{1,0:T(8,128)(2,1)S(1)}, u32[]{:S(2)}, u32[]{:S(2)}) collective-permute-start(bf16[128,512]{1,0:T(8,128)(2,1)S(1)} %pad_maximum_fusion.2), channel_id=1, source_target_pairs={{0,3},{1,0},{2,1},{3,2},{4,7},{5,4},{6,5},{7,6},{8,11},{9,8},{10,9... | collective-permute-start | bytes 393224 | tf_op jit(solution)/shard_map/ppermute | solution.py:130
  13.7 2.5 %collective-permute-done = bf16[128,512]{1,0:T(8,128)(2,1)S(1)} collective-permute-done((bf16[128,512]{1,0:T(8,128)(2,1)S(1)}, bf16[128,512]{1,0:T(8,128)(2,1)S(1)}, u32[]{:S(2)}, u32[]{:S(2)}) %collective-permute-start) | collective-permute-done | bytes 131104 | tf_op jit(solution)/shard_map/ppermute | solution.py:130
  16.2 4.5 %collective-permute-done.1 = bf16[128,512]{1,0:T(8,128)(2,1)S(1)} collective-permute-done((bf16[128,512]{1,0:T(8,128)(2,1)S(1)}, bf16[128,512]{1,0:T(8,128)(2,1)S(1)}, u32[]{:S(2)}, u32[]{:S(2)}) %collective-permute-start.1) | collective-permute-done | bytes 131104 | tf_op jit(solution)/shard_map/ppermute | solution.py:130
  20.7 0.0 collective-permute-done.2
  20.7 0.0 copy-start.2
  20.7 0.8 copy-done.2
  21.5 0.0 all-gather.2.cloned.1.call-update
  21.6 0.0 copy-done.3
  21.6 0.0 copy-start.7
  21.6 1.2 constant_dynamic-slice_fusion
  22.8 3.2 %collective-permute-start.3 = (bf16[128,2048]{1,0:T(8,128)(2,1)}, bf16[128,2048]{1,0:T(8,128)(2,1)S(1)}, u32[]{:S(2)}, u32[]{:S(2)}) collective-permute-start(bf16[128,2048]{1,0:T(8,128)(2,1)} %get-tuple-element.10), channel_id=1, source_target_pairs={{0,1},{1,2},{2,3},{3,0},{4,5},{5,6},{6,7},{7,4},{8,9},{9,10},{10,1... | collective-permute-start | bytes 1572872 | tf_op jit(solution)/shard_map/ppermute | solution.py:148
  26.0 1.1 collective-permute-start.7
  27.1 0.6 collective-permute-start.5
  27.7 0.0 copy-done.7
  27.7 0.1 fusion
  27.8 1.0 convert_reduce_fusion
  28.8 0.0 copy-start.8
  28.8 0.0 copy-start.9
  29.5 0.7 pad_add_fusion.1.meta_ref
  30.2 10.0 %collective-permute-done.3.q_ref = bf16[128,2048]{1,0:T(8,128)(2,1)S(1)} collective-permute-done((bf16[128,2048]{1,0:T(8,128)(2,1)}, bf16[128,2048]{1,0:T(8,128)(2,1)S(1)}, u32[]{:S(2)}, u32[]{:S(2)}) %collective-permute-start.3) | collective-permute-done | bytes 524320 | tf_op jit(solution)/shard_map/ppermute | solution.py:148
  40.2 19.2 %all-gather.2.cloned.1.call-done.k_ref.v_ref = bf16[4096,512]{1,0:T(8,128)(2,1)} async-done(((bf16[512,512]{1,0:T(8,128)(2,1)}), bf16[4096,512]{1,0:T(8,128)(2,1)}) %all-gather.2.cloned.1.call-update) | async-done | bytes 4194320 | tf_op jit(solution)/shard_map/all_gather | solution.py:132
  59.4 0.0 copy-done.11
  59.5 14.5 %shard_map.47 = bf16[128,2048]{1,0:T(8,128)(2,1)} custom-call(s32[3]{0:T(128)} %pad_add_fusion.1.meta_ref, s32[4096]{0:T(1024)} %doc_ref.7, bf16[128,2048]{1,0:T(8,128)(2,1)} %copy-done.6, bf16[4096,512]{1,0:T(8,128)(2,1)} %all-gather.2.cloned.1.call-done.k_ref.v_ref, bf16[4096,512]{1,0:T(8,128)(2,1)} %all-gather.2.cloned.1.call-done.k_ref.v_ref, ...), custom_call_target="tpu_custom_call" | custom-call | tf_op jit(solution)/shard_map/pallas_call | solution.py:94
  74.0 3.6 %collective-permute-start.4 = (bf16[128,2048]{1,0:T(8,128)(2,1)}, bf16[128,2048]{1,0:T(8,128)(2,1)S(1)}, u32[]{:S(2)}, u32[]{:S(2)}) collective-permute-start(bf16[128,2048]{1,0:T(8,128)(2,1)} %shard_map.47), channel_id=1, source_target_pairs={{0,3},{1,0},{2,1},{3,2},{4,7},{5,4},{6,5},{7,6},{8,11},{9,8},{10,9... | collective-permute-start | bytes 1572872 | tf_op jit(solution)/shard_map/ppermute | solution.py:152
  77.5 0.6 pad_add_fusion.3.meta_ref
  78.1 0.6 pad_add_fusion.2.meta_ref
  78.8 0.0 collective-permute-done.5.q_ref
  78.8 0.8 copy-done.5
  79.6 14.5 %shard_map.48 = bf16[128,2048]{1,0:T(8,128)(2,1)} custom-call(s32[3]{0:T(128)} %pad_add_fusion.2.meta_ref, s32[4096]{0:T(1024)} %doc_ref.7, bf16[128,2048]{1,0:T(8,128)(2,1)} %copy-done.5, bf16[4096,512]{1,0:T(8,128)(2,1)} %all-gather.2.cloned.1.call-done.k_ref.v_ref, bf16[4096,512]{1,0:T(8,128)(2,1)} %all-gather.2.cloned.1.call-done.k_ref.v_ref, ...), custom_call_target="tpu_custom_call" | custom-call | tf_op jit(solution)/shard_map/pallas_call | solution.py:94
  94.1 0.0 collective-permute-start.6
  94.1 0.6 pad_add_fusion.meta_ref
  94.7 0.0 collective-permute-done.7.q_ref
  94.7 0.8 copy-done.4
  95.5 14.7 %shard_map.49 = bf16[128,2048]{1,0:T(8,128)(2,1)} custom-call(s32[3]{0:T(128)} %pad_add_fusion.3.meta_ref, s32[4096]{0:T(1024)} %doc_ref.7, bf16[128,2048]{1,0:T(8,128)(2,1)} %copy-done.4, bf16[4096,512]{1,0:T(8,128)(2,1)} %all-gather.2.cloned.1.call-done.k_ref.v_ref, bf16[4096,512]{1,0:T(8,128)(2,1)} %all-gather.2.cloned.1.call-done.k_ref.v_ref, ...), custom_call_target="tpu_custom_call" | custom-call | tf_op jit(solution)/shard_map/pallas_call | solution.py:94
  110.2 1.1 collective-permute-start.8
  111.3 14.8 %shard_map.46 = bf16[128,2048]{1,0:T(8,128)(2,1)} custom-call(s32[3]{0:T(128)} %pad_add_fusion.meta_ref, s32[4096]{0:T(1024)} %doc_ref.7, bf16[128,2048]{1,0:T(8,128)(2,1)} %get-tuple-element.11.q_ref, bf16[4096,512]{1,0:T(8,128)(2,1)} %all-gather.2.cloned.1.call-done.k_ref.v_ref, bf16[4096,512]{1,0:T(8,128)(2,1)} %all-gather.2.cloned.1.call-done.k_ref.v_ref, ...), custom_call_target="tpu_custom_call" | custom-call | tf_op jit(solution)/shard_map/pallas_call | solution.py:94
  126.1 0.2 broadcast_in_dim.4
  126.3 0.8 copy-done.1
  127.2 0.0 collective-permute-done.4
  127.2 2.4 %collective-permute-done.6 = bf16[128,2048]{1,0:T(8,128)(2,1)S(1)} collective-permute-done((bf16[128,2048]{1,0:T(8,128)(2,1)}, bf16[128,2048]{1,0:T(8,128)(2,1)S(1)}, u32[]{:S(2)}, u32[]{:S(2)}) %collective-permute-start.6) | collective-permute-done | bytes 524320 | tf_op jit(solution)/shard_map/ppermute | solution.py:152
  129.7 0.0 copy-start
  129.7 0.0 collective-permute-done.8
  129.7 1.3 copy-done
  131.0 0.8 constant_dynamic-update-slice_fusion
  (22 shorter events, 0.3 us)
Async XLA Ops:
  6.5 52.9 %all-gather.2.cloned.1.call-start = ((), (), s32[]{:S(2)}) async-start(), calls=%async_computation | async-start | bytes 4718592 | tf_op jit(solution)/shard_map/all_gather | solution.py:132
  6.5 15.1 %copy-start.3 = (bf16[128,8192]{1,0:T(8,128)(2,1)S(1)}, bf16[128,8192]{1,0:T(8,128)(2,1)}, u32[]{:S(2)}) copy-start(bf16[128,8192]{1,0:T(8,128)(2,1)} %param.4) | copy-start | bytes 6291460
  7.8 8.3 %collective-permute-start = (bf16[128,512]{1,0:T(8,128)(2,1)S(1)}, bf16[128,512]{1,0:T(8,128)(2,1)S(1)}, u32[]{:S(2)}, u32[]{:S(2)}) collective-permute-start(bf16[128,512]{1,0:T(8,128)(2,1)S(1)} %pad_maximum_fusion), channel_id=1, source_target_pairs={{0,1},{1,2},{2,3},{3,0},{4,5},{5,6},{6,7},{7,4},{8,9},{9,10},{10,1... | collective-permute-start | bytes 393224 | tf_op jit(solution)/shard_map/ppermute | solution.py:130
  9.5 11.2 %collective-permute-start.1 = (bf16[128,512]{1,0:T(8,128)(2,1)S(1)}, bf16[128,512]{1,0:T(8,128)(2,1)S(1)}, u32[]{:S(2)}, u32[]{:S(2)}) collective-permute-start(bf16[128,512]{1,0:T(8,128)(2,1)S(1)} %pad_maximum_fusion.1), channel_id=1, source_target_pairs={{0,2},{1,3},{2,0},{3,1},{4,6},{5,7},{6,4},{7,5},{8,10},{9,11},{10,... | collective-permute-start | bytes 393224 | tf_op jit(solution)/shard_map/ppermute | solution.py:130
  12.1 8.6 %collective-permute-start.2 = (bf16[128,512]{1,0:T(8,128)(2,1)S(1)}, bf16[128,512]{1,0:T(8,128)(2,1)S(1)}, u32[]{:S(2)}, u32[]{:S(2)}) collective-permute-start(bf16[128,512]{1,0:T(8,128)(2,1)S(1)} %pad_maximum_fusion.2), channel_id=1, source_target_pairs={{0,3},{1,0},{2,1},{3,2},{4,7},{5,4},{6,5},{7,6},{8,11},{9,8},{10,9... | collective-permute-start | bytes 393224 | tf_op jit(solution)/shard_map/ppermute | solution.py:130
  20.7 0.8 copy-start.2
  21.6 6.1 %copy-start.7 = (s32[4096]{0:T(1024)S(1)}, s32[4096]{0:T(1024)}, u32[]{:S(2)}) copy-start(s32[4096]{0:T(1024)} %doc_ref.7) | copy-start | bytes 49156
  22.8 17.4 %collective-permute-start.3 = (bf16[128,2048]{1,0:T(8,128)(2,1)}, bf16[128,2048]{1,0:T(8,128)(2,1)S(1)}, u32[]{:S(2)}, u32[]{:S(2)}) collective-permute-start(bf16[128,2048]{1,0:T(8,128)(2,1)} %get-tuple-element.10), channel_id=1, source_target_pairs={{0,1},{1,2},{2,3},{3,0},{4,5},{5,6},{6,7},{7,4},{8,9},{9,10},{10,1... | collective-permute-start | bytes 1572872 | tf_op jit(solution)/shard_map/ppermute | solution.py:148
  26.0 68.6 %collective-permute-start.7 = (bf16[128,2048]{1,0:T(8,128)(2,1)S(1)}, bf16[128,2048]{1,0:T(8,128)(2,1)S(1)}, u32[]{:S(2)}, u32[]{:S(2)}) collective-permute-start(bf16[128,2048]{1,0:T(8,128)(2,1)S(1)} %get-tuple-element.9), channel_id=1, source_target_pairs={{0,3},{1,0},{2,1},{3,2},{4,7},{5,4},{6,5},{7,6},{8,11},{9,8},{10,9... | collective-permute-start | bytes 1572872 | tf_op jit(solution)/shard_map/ppermute | solution.py:148
  27.1 51.6 %collective-permute-start.5 = (bf16[128,2048]{1,0:T(8,128)(2,1)S(1)}, bf16[128,2048]{1,0:T(8,128)(2,1)S(1)}, u32[]{:S(2)}, u32[]{:S(2)}) collective-permute-start(bf16[128,2048]{1,0:T(8,128)(2,1)S(1)} %get-tuple-element.12), channel_id=1, source_target_pairs={{0,2},{1,3},{2,0},{3,1},{4,6},{5,7},{6,4},{7,5},{8,10},{9,11},{10,... | collective-permute-start | bytes 1572872 | tf_op jit(solution)/shard_map/ppermute | solution.py:148
  28.8 30.7 %copy-start.11 = (s32[128]{0:T(128)}, s32[128]{0:T(128)S(1)}, u32[]{:S(2)}) copy-start(s32[128]{0:T(128)S(1)} %get-tuple-element.6) | copy-start | bytes 1540
  28.8 45.2 %copy-start.8 = (s32[128]{0:T(128)}, s32[128]{0:T(128)S(1)}, u32[]{:S(2)}) copy-start(s32[128]{0:T(128)S(1)} %get-tuple-element.8) | copy-start | bytes 1540
  28.8 45.2 %copy-start.9 = (s32[128]{0:T(128)}, s32[128]{0:T(128)S(1)}, u32[]{:S(2)}) copy-start(s32[128]{0:T(128)S(1)} %get-tuple-element.5) | copy-start | bytes 1540
  28.8 45.2 %copy-start.10 = (s32[128]{0:T(128)}, s32[128]{0:T(128)S(1)}, u32[]{:S(2)}) copy-start(s32[128]{0:T(128)S(1)} %get-tuple-element.7) | copy-start | bytes 1540
  40.2 19.2 %copy-start.6 = (bf16[128,2048]{1,0:T(8,128)(2,1)}, bf16[128,2048]{1,0:T(8,128)(2,1)S(1)}, u32[]{:S(2)}) copy-start(bf16[128,2048]{1,0:T(8,128)(2,1)S(1)} %collective-permute-done.3.q_ref) | copy-start | bytes 1572868
  74.0 53.2 %collective-permute-start.4 = (bf16[128,2048]{1,0:T(8,128)(2,1)}, bf16[128,2048]{1,0:T(8,128)(2,1)S(1)}, u32[]{:S(2)}, u32[]{:S(2)}) collective-permute-start(bf16[128,2048]{1,0:T(8,128)(2,1)} %shard_map.47), channel_id=1, source_target_pairs={{0,3},{1,0},{2,1},{3,2},{4,7},{5,4},{6,5},{7,6},{8,11},{9,8},{10,9... | collective-permute-start | bytes 1572872 | tf_op jit(solution)/shard_map/ppermute | solution.py:152
  78.8 0.8 copy-start.5
  94.1 35.5 %collective-permute-start.6 = (bf16[128,2048]{1,0:T(8,128)(2,1)}, bf16[128,2048]{1,0:T(8,128)(2,1)S(1)}, u32[]{:S(2)}, u32[]{:S(2)}) collective-permute-start(bf16[128,2048]{1,0:T(8,128)(2,1)} %shard_map.48), channel_id=1, source_target_pairs={{0,2},{1,3},{2,0},{3,1},{4,6},{5,7},{6,4},{7,5},{8,10},{9,11},{10,... | collective-permute-start | bytes 1572872 | tf_op jit(solution)/shard_map/ppermute | solution.py:152
  94.7 0.8 copy-start.4
  110.2 19.5 %collective-permute-start.8 = (bf16[128,2048]{1,0:T(8,128)(2,1)}, bf16[128,2048]{1,0:T(8,128)(2,1)S(1)}, u32[]{:S(2)}, u32[]{:S(2)}) collective-permute-start(bf16[128,2048]{1,0:T(8,128)(2,1)} %shard_map.49), channel_id=1, source_target_pairs={{0,1},{1,2},{2,3},{3,0},{4,5},{5,6},{6,7},{7,4},{8,9},{9,10},{10,1... | collective-permute-start | bytes 1572872 | tf_op jit(solution)/shard_map/ppermute | solution.py:152
  126.1 1.0 copy-start.1
  129.7 1.3 copy-start
Sparse Core Ops, SparseCore 0:
  21.7 37.7 all-gather.1

commit v5 on v0

--- a/solution.py
+++ b/solution.py
@@ -69,7 +69,7 @@
     def _():
         for j in range(groups * heads_per):
             cols = slice(j * HEAD_DIM, (j + 1) * HEAD_DIM)
-            o_ref[:, cols] = (acc_sc[j] / l_sc[j]).T.astype(o_ref.dtype)
+            o_ref[:, cols] = (acc_sc[j] * (1.0 / l_sc[j])).T.astype(o_ref.dtype)
 
 
 def attend(q_tile, q_off, kv_rows, doc_ids, groups, heads_per):

time: 135 us -> 139 us (1.030); the launches traced: 132 us -> 139 us
  Pallas kernels: 43 us -> 56.1 us
  waiting for transfers between devices: 47.5 us -> 41 us
    pallas_call x4, Pallas kernels: 43 us -> 56.1 us  [attend(): pl.pallas_call(kernel, out_shape=jax.ShapeDtypeStruct((q_rows, width), jn...]
    ppermute x3, waiting for transfers between devices: 11.2 us -> 4.69 us  [body(): lax.ppermute(out_tile, 'head', [(i, (i - t) % head_count) for i in range(...]
  transfers between devices with their start and end apart: 10 -> 10, of which waited for: 5 -> 5; matrix products, arithmetic and copies ran while one was open for 4% -> 4% of each run, Pallas kernels for 33% -> 41%
where the time goes in v5:
time: 139 us
  Pallas kernels  56.1 us (40%)
  waiting for transfers between devices  41 us (29%)
  starting transfers between devices  15.3 us (11%)
  between operations  14.4 us (10%)
  local copies, waits for them, and re-layouts  8.31 us (6%)
  other arithmetic  3.52 us (3%)
    pallas_call x4, Pallas kernels, attend(): pl.pallas_call(kernel, out_shape=jax.ShapeDtypeStruct((q_rows, width), jn...  56.1 us
    all_gather x1, waiting for transfers between devices, gather_kv(): return lax.all_gather(local, 'seq', axis=0, tiled=True)  19.2 us
    ppermute x3, waiting for transfers between devices, body(): lax.ppermute(piece, 'head', [(i, (i + t) % head_count) for i in range(hea...  10 us
    ppermute x3, waiting for transfers between devices, gather_kv(): lax.ppermute(piece, 'head', [(i, (i + t) % head_count) for i in range(hea...  7.01 us
    ppermute x3, starting transfers between devices, gather_kv(): lax.ppermute(piece, 'head', [(i, (i + t) % head_count) for i in range(hea...  5.68 us
    ppermute x3, starting transfers between devices, body(): lax.ppermute(piece, 'head', [(i, (i + t) % head_count) for i in range(hea...  4.91 us
    ppermute x3, waiting for transfers between devices, body(): lax.ppermute(out_tile, 'head', [(i, (i - t) % head_count) for i in range(...  4.69 us
    ppermute x3, starting transfers between devices, body(): lax.ppermute(out_tile, 'head', [(i, (i - t) % head_count) for i in range(...  4.67 us
  transfers between devices with their start and end apart: 10, of which 5 were waited for; matrix products, arithmetic and copies ran while one was open for 4% of the time, Pallas kernels for 41%

profile of v5, /device:TPU:6, one launch (start us, length us, event | category | flops | bytes accessed | tf_op | source)
XLA Modules:
  0.0 138.6 jit_solution(1236729310964325999)
XLA Ops:
  6.5 0.0 all-gather.2.cloned.1.call-start
  6.5 1.3 constant_dynamic-slice_fusion.3
  7.8 1.6 %collective-permute-start = (bf16[128,512]{1,0:T(8,128)(2,1)S(1)}, bf16[128,512]{1,0:T(8,128)(2,1)S(1)}, u32[]{:S(2)}, u32[]{:S(2)}) collective-permute-start(bf16[128,512]{1,0:T(8,128)(2,1)S(1)} %pad_maximum_fusion), channel_id=1, source_target_pairs={{0,1},{1,2},{2,3},{3,0},{4,5},{5,6},{6,7},{7,4},{8,9},{9,10},{10,1... | collective-permute-start | bytes 393224 | tf_op jit(solution)/shard_map/ppermute | solution.py:130
  9.5 2.7 %collective-permute-start.1 = (bf16[128,512]{1,0:T(8,128)(2,1)S(1)}, bf16[128,512]{1,0:T(8,128)(2,1)S(1)}, u32[]{:S(2)}, u32[]{:S(2)}) collective-permute-start(bf16[128,512]{1,0:T(8,128)(2,1)S(1)} %pad_maximum_fusion.1), channel_id=1, source_target_pairs={{0,2},{1,3},{2,0},{3,1},{4,6},{5,7},{6,4},{7,5},{8,10},{9,11},{10,... | collective-permute-start | bytes 393224 | tf_op jit(solution)/shard_map/ppermute | solution.py:130
  12.1 1.4 %collective-permute-start.2 = (bf16[128,512]{1,0:T(8,128)(2,1)S(1)}, bf16[128,512]{1,0:T(8,128)(2,1)S(1)}, u32[]{:S(2)}, u32[]{:S(2)}) collective-permute-start(bf16[128,512]{1,0:T(8,128)(2,1)S(1)} %pad_maximum_fusion.2), channel_id=1, source_target_pairs={{0,3},{1,0},{2,1},{3,2},{4,7},{5,4},{6,5},{7,6},{8,11},{9,8},{10,9... | collective-permute-start | bytes 393224 | tf_op jit(solution)/shard_map/ppermute | solution.py:130
  13.7 2.5 %collective-permute-done = bf16[128,512]{1,0:T(8,128)(2,1)S(1)} collective-permute-done((bf16[128,512]{1,0:T(8,128)(2,1)S(1)}, bf16[128,512]{1,0:T(8,128)(2,1)S(1)}, u32[]{:S(2)}, u32[]{:S(2)}) %collective-permute-start) | collective-permute-done | bytes 131104 | tf_op jit(solution)/shard_map/ppermute | solution.py:130
  16.2 4.5 %collective-permute-done.1 = bf16[128,512]{1,0:T(8,128)(2,1)S(1)} collective-permute-done((bf16[128,512]{1,0:T(8,128)(2,1)S(1)}, bf16[128,512]{1,0:T(8,128)(2,1)S(1)}, u32[]{:S(2)}, u32[]{:S(2)}) %collective-permute-start.1) | collective-permute-done | bytes 131104 | tf_op jit(solution)/shard_map/ppermute | solution.py:130
  20.7 0.0 collective-permute-done.2
  20.7 0.0 copy-start.2
  20.7 0.8 copy-done.2
  21.5 0.0 all-gather.2.cloned.1.call-update
  21.6 0.0 copy-done.3
  21.6 0.0 copy-start.7
  21.6 1.2 constant_dynamic-slice_fusion
  22.8 3.2 %collective-permute-start.3 = (bf16[128,2048]{1,0:T(8,128)(2,1)}, bf16[128,2048]{1,0:T(8,128)(2,1)S(1)}, u32[]{:S(2)}, u32[]{:S(2)}) collective-permute-start(bf16[128,2048]{1,0:T(8,128)(2,1)} %get-tuple-element.10), channel_id=1, source_target_pairs={{0,1},{1,2},{2,3},{3,0},{4,5},{5,6},{6,7},{7,4},{8,9},{9,10},{10,1... | collective-permute-start | bytes 1572872 | tf_op jit(solution)/shard_map/ppermute | solution.py:148
  26.0 1.1 collective-permute-start.7
  27.1 0.6 collective-permute-start.5
  27.7 0.0 copy-done.7
  27.7 0.1 fusion
  27.8 1.0 convert_reduce_fusion
  28.8 0.0 copy-start.8
  28.8 0.0 copy-start.9
  29.5 0.7 pad_add_fusion.1.meta_ref
  30.2 10.0 %collective-permute-done.3.q_ref = bf16[128,2048]{1,0:T(8,128)(2,1)S(1)} collective-permute-done((bf16[128,2048]{1,0:T(8,128)(2,1)}, bf16[128,2048]{1,0:T(8,128)(2,1)S(1)}, u32[]{:S(2)}, u32[]{:S(2)}) %collective-permute-start.3) | collective-permute-done | bytes 524320 | tf_op jit(solution)/shard_map/ppermute | solution.py:148
  40.2 19.2 %all-gather.2.cloned.1.call-done.k_ref.v_ref = bf16[4096,512]{1,0:T(8,128)(2,1)} async-done(((bf16[512,512]{1,0:T(8,128)(2,1)}), bf16[4096,512]{1,0:T(8,128)(2,1)}) %all-gather.2.cloned.1.call-update) | async-done | bytes 4194320 | tf_op jit(solution)/shard_map/all_gather | solution.py:132
  59.5 14.0 %shard_map.47 = bf16[128,2048]{1,0:T(8,128)(2,1)} custom-call(s32[3]{0:T(128)} %pad_add_fusion.1.meta_ref, s32[4096]{0:T(1024)} %doc_ref.7, bf16[128,2048]{1,0:T(8,128)(2,1)} %copy-done.6, bf16[4096,512]{1,0:T(8,128)(2,1)} %all-gather.2.cloned.1.call-done.k_ref.v_ref, bf16[4096,512]{1,0:T(8,128)(2,1)} %all-gather.2.cloned.1.call-done.k_ref.v_ref, ...), custom_call_target="tpu_custom_call" | custom-call | tf_op jit(solution)/shard_map/pallas_call | solution.py:94
  73.5 0.0 copy-done.8
  73.5 3.6 %collective-permute-start.4 = (bf16[128,2048]{1,0:T(8,128)(2,1)}, bf16[128,2048]{1,0:T(8,128)(2,1)S(1)}, u32[]{:S(2)}, u32[]{:S(2)}) collective-permute-start(bf16[128,2048]{1,0:T(8,128)(2,1)} %shard_map.47), channel_id=1, source_target_pairs={{0,3},{1,0},{2,1},{3,2},{4,7},{5,4},{6,5},{7,6},{8,11},{9,8},{10,9... | collective-permute-start | bytes 1572872 | tf_op jit(solution)/shard_map/ppermute | solution.py:152
  77.1 0.6 pad_add_fusion.3.meta_ref
  77.7 0.6 pad_add_fusion.2.meta_ref
  78.3 0.0 collective-permute-done.5.q_ref
  78.3 0.8 copy-done.5
  79.1 14.1 %shard_map.48 = bf16[128,2048]{1,0:T(8,128)(2,1)} custom-call(s32[3]{0:T(128)} %pad_add_fusion.2.meta_ref, s32[4096]{0:T(1024)} %doc_ref.7, bf16[128,2048]{1,0:T(8,128)(2,1)} %copy-done.5, bf16[4096,512]{1,0:T(8,128)(2,1)} %all-gather.2.cloned.1.call-done.k_ref.v_ref, bf16[4096,512]{1,0:T(8,128)(2,1)} %all-gather.2.cloned.1.call-done.k_ref.v_ref, ...), custom_call_target="tpu_custom_call" | custom-call | tf_op jit(solution)/shard_map/pallas_call | solution.py:94
  93.1 0.0 collective-permute-start.6
  93.1 0.6 pad_add_fusion.meta_ref
  93.7 0.0 collective-permute-done.7.q_ref
  93.8 0.8 copy-done.4
  94.5 14.0 %shard_map.49 = bf16[128,2048]{1,0:T(8,128)(2,1)} custom-call(s32[3]{0:T(128)} %pad_add_fusion.3.meta_ref, s32[4096]{0:T(1024)} %doc_ref.7, bf16[128,2048]{1,0:T(8,128)(2,1)} %copy-done.4, bf16[4096,512]{1,0:T(8,128)(2,1)} %all-gather.2.cloned.1.call-done.k_ref.v_ref, bf16[4096,512]{1,0:T(8,128)(2,1)} %all-gather.2.cloned.1.call-done.k_ref.v_ref, ...), custom_call_target="tpu_custom_call" | custom-call | tf_op jit(solution)/shard_map/pallas_call | solution.py:94
  108.6 1.1 collective-permute-start.8
  109.7 14.0 %shard_map.46 = bf16[128,2048]{1,0:T(8,128)(2,1)} custom-call(s32[3]{0:T(128)} %pad_add_fusion.meta_ref, s32[4096]{0:T(1024)} %doc_ref.7, bf16[128,2048]{1,0:T(8,128)(2,1)} %get-tuple-element.11.q_ref, bf16[4096,512]{1,0:T(8,128)(2,1)} %all-gather.2.cloned.1.call-done.k_ref.v_ref, bf16[4096,512]{1,0:T(8,128)(2,1)} %all-gather.2.cloned.1.call-done.k_ref.v_ref, ...), custom_call_target="tpu_custom_call" | custom-call | tf_op jit(solution)/shard_map/pallas_call | solution.py:94
  123.7 0.2 broadcast_in_dim.4
  123.9 0.8 copy-done.1
  124.8 0.0 collective-permute-done.4
  124.9 4.7 %collective-permute-done.6 = bf16[128,2048]{1,0:T(8,128)(2,1)S(1)} collective-permute-done((bf16[128,2048]{1,0:T(8,128)(2,1)}, bf16[128,2048]{1,0:T(8,128)(2,1)S(1)}, u32[]{:S(2)}, u32[]{:S(2)}) %collective-permute-start.6) | collective-permute-done | bytes 524320 | tf_op jit(solution)/shard_map/ppermute | solution.py:152
  129.6 0.0 copy-start
  129.6 0.0 collective-permute-done.8
  129.6 1.3 copy-done
  130.9 0.8 constant_dynamic-update-slice_fusion
  (22 shorter events, 0.3 us)
Async XLA Ops:
  6.5 52.9 %all-gather.2.cloned.1.call-start = ((), (), s32[]{:S(2)}) async-start(), calls=%async_computation | async-start | bytes 4718592 | tf_op jit(solution)/shard_map/all_gather | solution.py:132
  6.5 15.1 %copy-start.3 = (bf16[128,8192]{1,0:T(8,128)(2,1)S(1)}, bf16[128,8192]{1,0:T(8,128)(2,1)}, u32[]{:S(2)}) copy-start(bf16[128,8192]{1,0:T(8,128)(2,1)} %param.4) | copy-start | bytes 6291460
  7.8 8.3 %collective-permute-start = (bf16[128,512]{1,0:T(8,128)(2,1)S(1)}, bf16[128,512]{1,0:T(8,128)(2,1)S(1)}, u32[]{:S(2)}, u32[]{:S(2)}) collective-permute-start(bf16[128,512]{1,0:T(8,128)(2,1)S(1)} %pad_maximum_fusion), channel_id=1, source_target_pairs={{0,1},{1,2},{2,3},{3,0},{4,5},{5,6},{6,7},{7,4},{8,9},{9,10},{10,1... | collective-permute-start | bytes 393224 | tf_op jit(solution)/shard_map/ppermute | solution.py:130
  9.5 11.2 %collective-permute-start.1 = (bf16[128,512]{1,0:T(8,128)(2,1)S(1)}, bf16[128,512]{1,0:T(8,128)(2,1)S(1)}, u32[]{:S(2)}, u32[]{:S(2)}) collective-permute-start(bf16[128,512]{1,0:T(8,128)(2,1)S(1)} %pad_maximum_fusion.1), channel_id=1, source_target_pairs={{0,2},{1,3},{2,0},{3,1},{4,6},{5,7},{6,4},{7,5},{8,10},{9,11},{10,... | collective-permute-start | bytes 393224 | tf_op jit(solution)/shard_map/ppermute | solution.py:130
  12.1 8.6 %collective-permute-start.2 = (bf16[128,512]{1,0:T(8,128)(2,1)S(1)}, bf16[128,512]{1,0:T(8,128)(2,1)S(1)}, u32[]{:S(2)}, u32[]{:S(2)}) collective-permute-start(bf16[128,512]{1,0:T(8,128)(2,1)S(1)} %pad_maximum_fusion.2), channel_id=1, source_target_pairs={{0,3},{1,0},{2,1},{3,2},{4,7},{5,4},{6,5},{7,6},{8,11},{9,8},{10,9... | collective-permute-start | bytes 393224 | tf_op jit(solution)/shard_map/ppermute | solution.py:130
  20.7 0.8 copy-start.2
  21.6 6.1 %copy-start.7 = (s32[4096]{0:T(1024)S(1)}, s32[4096]{0:T(1024)}, u32[]{:S(2)}) copy-start(s32[4096]{0:T(1024)} %doc_ref.7) | copy-start | bytes 49156
  22.8 17.4 %collective-permute-start.3 = (bf16[128,2048]{1,0:T(8,128)(2,1)}, bf16[128,2048]{1,0:T(8,128)(2,1)S(1)}, u32[]{:S(2)}, u32[]{:S(2)}) collective-permute-start(bf16[128,2048]{1,0:T(8,128)(2,1)} %get-tuple-element.10), channel_id=1, source_target_pairs={{0,1},{1,2},{2,3},{3,0},{4,5},{5,6},{6,7},{7,4},{8,9},{9,10},{10,1... | collective-permute-start | bytes 1572872 | tf_op jit(solution)/shard_map/ppermute | solution.py:148
  26.0 67.7 %collective-permute-start.7 = (bf16[128,2048]{1,0:T(8,128)(2,1)S(1)}, bf16[128,2048]{1,0:T(8,128)(2,1)S(1)}, u32[]{:S(2)}, u32[]{:S(2)}) collective-permute-start(bf16[128,2048]{1,0:T(8,128)(2,1)S(1)} %get-tuple-element.9), channel_id=1, source_target_pairs={{0,3},{1,0},{2,1},{3,2},{4,7},{5,4},{6,5},{7,6},{8,11},{9,8},{10,9... | collective-permute-start | bytes 1572872 | tf_op jit(solution)/shard_map/ppermute | solution.py:148
  27.1 51.2 %collective-permute-start.5 = (bf16[128,2048]{1,0:T(8,128)(2,1)S(1)}, bf16[128,2048]{1,0:T(8,128)(2,1)S(1)}, u32[]{:S(2)}, u32[]{:S(2)}) collective-permute-start(bf16[128,2048]{1,0:T(8,128)(2,1)S(1)} %get-tuple-element.12), channel_id=1, source_target_pairs={{0,2},{1,3},{2,0},{3,1},{4,6},{5,7},{6,4},{7,5},{8,10},{9,11},{10,... | collective-permute-start | bytes 1572872 | tf_op jit(solution)/shard_map/ppermute | solution.py:148
  28.8 30.7 %copy-start.11 = (s32[128]{0:T(128)}, s32[128]{0:T(128)S(1)}, u32[]{:S(2)}) copy-start(s32[128]{0:T(128)S(1)} %get-tuple-element.6) | copy-start | bytes 1540
  28.8 44.7 %copy-start.8 = (s32[128]{0:T(128)}, s32[128]{0:T(128)S(1)}, u32[]{:S(2)}) copy-start(s32[128]{0:T(128)S(1)} %get-tuple-element.8) | copy-start | bytes 1540
  28.8 44.7 %copy-start.9 = (s32[128]{0:T(128)}, s32[128]{0:T(128)S(1)}, u32[]{:S(2)}) copy-start(s32[128]{0:T(128)S(1)} %get-tuple-element.5) | copy-start | bytes 1540
  28.8 44.7 %copy-start.10 = (s32[128]{0:T(128)}, s32[128]{0:T(128)S(1)}, u32[]{:S(2)}) copy-start(s32[128]{0:T(128)S(1)} %get-tuple-element.7) | copy-start | bytes 1540
  40.2 19.2 %copy-start.6 = (bf16[128,2048]{1,0:T(8,128)(2,1)}, bf16[128,2048]{1,0:T(8,128)(2,1)S(1)}, u32[]{:S(2)}) copy-start(bf16[128,2048]{1,0:T(8,128)(2,1)S(1)} %collective-permute-done.3.q_ref) | copy-start | bytes 1572868
  73.5 51.3 %collective-permute-start.4 = (bf16[128,2048]{1,0:T(8,128)(2,1)}, bf16[128,2048]{1,0:T(8,128)(2,1)S(1)}, u32[]{:S(2)}, u32[]{:S(2)}) collective-permute-start(bf16[128,2048]{1,0:T(8,128)(2,1)} %shard_map.47), channel_id=1, source_target_pairs={{0,3},{1,0},{2,1},{3,2},{4,7},{5,4},{6,5},{7,6},{8,11},{9,8},{10,9... | collective-permute-start | bytes 1572872 | tf_op jit(solution)/shard_map/ppermute | solution.py:152
  78.3 0.8 copy-start.5
  93.1 36.4 %collective-permute-start.6 = (bf16[128,2048]{1,0:T(8,128)(2,1)}, bf16[128,2048]{1,0:T(8,128)(2,1)S(1)}, u32[]{:S(2)}, u32[]{:S(2)}) collective-permute-start(bf16[128,2048]{1,0:T(8,128)(2,1)} %shard_map.48), channel_id=1, source_target_pairs={{0,2},{1,3},{2,0},{3,1},{4,6},{5,7},{6,4},{7,5},{8,10},{9,11},{10,... | collective-permute-start | bytes 1572872 | tf_op jit(solution)/shard_map/ppermute | solution.py:152
  93.8 0.8 copy-start.4
  108.6 21.0 %collective-permute-start.8 = (bf16[128,2048]{1,0:T(8,128)(2,1)}, bf16[128,2048]{1,0:T(8,128)(2,1)S(1)}, u32[]{:S(2)}, u32[]{:S(2)}) collective-permute-start(bf16[128,2048]{1,0:T(8,128)(2,1)} %shard_map.49), channel_id=1, source_target_pairs={{0,1},{1,2},{2,3},{3,0},{4,5},{5,6},{6,7},{7,4},{8,9},{9,10},{10,1... | collective-permute-start | bytes 1572872 | tf_op jit(solution)/shard_map/ppermute | solution.py:152
  123.7 1.0 copy-start.1
  129.6 1.3 copy-start
Sparse Core Ops, SparseCore 0:
  21.7 37.7 all-gather.1

commit v6 on v5

--- a/solution.py
+++ b/solution.py
@@ -69,7 +69,7 @@
     def _():
         for j in range(groups * heads_per):
             cols = slice(j * HEAD_DIM, (j + 1) * HEAD_DIM)
-            o_ref[:, cols] = (acc_sc[j] * (1.0 / l_sc[j])).T.astype(o_ref.dtype)
+            o_ref[:, cols] = (acc_sc[j] * (1.0 / l_sc[j])).astype(o_ref.dtype).T
 
 
 def attend(q_tile, q_off, kv_rows, doc_ids, groups, heads_per):

time: 139 us -> 139 us (level); the launches traced: 139 us -> 141 us
  starting transfers between devices: 15.3 us -> 25.5 us
  waiting for transfers between devices: 41 us -> 36.3 us
  Pallas kernels: 56.1 us -> 53.1 us
    ppermute x3, starting transfers between devices: 4.67 us -> 14.9 us  [body(): lax.ppermute(out_tile, 'head', [(i, (i - t) % head_count) for i in range(...]
    ppermute x3, waiting for transfers between devices: 4.69 us -> 0.01 us  [body(): lax.ppermute(out_tile, 'head', [(i, (i - t) % head_count) for i in range(...]
    pallas_call x4, Pallas kernels: 56.1 us -> 53.1 us  [attend(): pl.pallas_call(kernel, out_shape=jax.ShapeDtypeStruct((q_rows, width), jn...]
  transfers between devices with their start and end apart: 10 -> 10, of which waited for: 5 -> 4; matrix products, arithmetic and copies ran while one was open for 4% -> 4% of each run, Pallas kernels for 41% -> 38%
where the time goes in v6:
time: 139 us; the launch traced here: 141 us
  Pallas kernels  53.1 us (38%)
  waiting for transfers between devices  36.3 us (26%)
  starting transfers between devices  25.5 us (18%)
  between operations  14.4 us (10%)
  local copies, waits for them, and re-layouts  8.32 us (6%)
  other arithmetic  3.52 us (3%)
    pallas_call x4, Pallas kernels, attend(): pl.pallas_call(kernel, out_shape=jax.ShapeDtypeStruct((q_rows, width), jn...  53.1 us
    all_gather x1, waiting for transfers between devices, gather_kv(): return lax.all_gather(local, 'seq', axis=0, tiled=True)  19.2 us
    ppermute x3, starting transfers between devices, body(): lax.ppermute(out_tile, 'head', [(i, (i - t) % head_count) for i in range(...  14.9 us
    ppermute x3, waiting for transfers between devices, body(): lax.ppermute(piece, 'head', [(i, (i + t) % head_count) for i in range(hea...  10 us
    ppermute x3, waiting for transfers between devices, gather_kv(): lax.ppermute(piece, 'head', [(i, (i + t) % head_count) for i in range(hea...  7.01 us
    ppermute x3, starting transfers between devices, gather_kv(): lax.ppermute(piece, 'head', [(i, (i + t) % head_count) for i in range(hea...  5.68 us
    ppermute x3, starting transfers between devices, body(): lax.ppermute(piece, 'head', [(i, (i + t) % head_count) for i in range(hea...  4.91 us
    unnamed x24, local copies, waits for them, and re-layouts  4.55 us
  transfers between devices with their start and end apart: 10, of which 4 were waited for; matrix products, arithmetic and copies ran while one was open for 4% of the time, Pallas kernels for 38%

profile of v6, /device:TPU:6, one launch (start us, length us, event | category | flops | bytes accessed | tf_op | source)
XLA Modules:
  0.0 141.1 jit_solution(13158035911786437300)
XLA Ops:
  6.5 0.0 all-gather.2.cloned.1.call-start
  6.5 1.3 constant_dynamic-slice_fusion.3
  7.8 1.6 %collective-permute-start = (bf16[128,512]{1,0:T(8,128)(2,1)S(1)}, bf16[128,512]{1,0:T(8,128)(2,1)S(1)}, u32[]{:S(2)}, u32[]{:S(2)}) collective-permute-start(bf16[128,512]{1,0:T(8,128)(2,1)S(1)} %pad_maximum_fusion), channel_id=1, source_target_pairs={{0,1},{1,2},{2,3},{3,0},{4,5},{5,6},{6,7},{7,4},{8,9},{9,10},{10,1... | collective-permute-start | bytes 393224 | tf_op jit(solution)/shard_map/ppermute | solution.py:130
  9.5 2.7 %collective-permute-start.1 = (bf16[128,512]{1,0:T(8,128)(2,1)S(1)}, bf16[128,512]{1,0:T(8,128)(2,1)S(1)}, u32[]{:S(2)}, u32[]{:S(2)}) collective-permute-start(bf16[128,512]{1,0:T(8,128)(2,1)S(1)} %pad_maximum_fusion.1), channel_id=1, source_target_pairs={{0,2},{1,3},{2,0},{3,1},{4,6},{5,7},{6,4},{7,5},{8,10},{9,11},{10,... | collective-permute-start | bytes 393224 | tf_op jit(solution)/shard_map/ppermute | solution.py:130
  12.1 1.4 collective-permute-start.2
  13.7 2.5 %collective-permute-done = bf16[128,512]{1,0:T(8,128)(2,1)S(1)} collective-permute-done((bf16[128,512]{1,0:T(8,128)(2,1)S(1)}, bf16[128,512]{1,0:T(8,128)(2,1)S(1)}, u32[]{:S(2)}, u32[]{:S(2)}) %collective-permute-start) | collective-permute-done | bytes 131104 | tf_op jit(solution)/shard_map/ppermute | solution.py:130
  16.2 4.5 %collective-permute-done.1 = bf16[128,512]{1,0:T(8,128)(2,1)S(1)} collective-permute-done((bf16[128,512]{1,0:T(8,128)(2,1)S(1)}, bf16[128,512]{1,0:T(8,128)(2,1)S(1)}, u32[]{:S(2)}, u32[]{:S(2)}) %collective-permute-start.1) | collective-permute-done | bytes 131104 | tf_op jit(solution)/shard_map/ppermute | solution.py:130
  20.7 0.0 collective-permute-done.2
  20.7 0.0 copy-start.2
  20.7 0.8 copy-done.2
  21.5 0.0 all-gather.2.cloned.1.call-update
  21.6 0.0 copy-done.3
  21.6 0.0 copy-start.7
  21.6 1.2 constant_dynamic-slice_fusion
  22.8 3.2 %collective-permute-start.3 = (bf16[128,2048]{1,0:T(8,128)(2,1)}, bf16[128,2048]{1,0:T(8,128)(2,1)S(1)}, u32[]{:S(2)}, u32[]{:S(2)}) collective-permute-start(bf16[128,2048]{1,0:T(8,128)(2,1)} %get-tuple-element.10), channel_id=1, source_target_pairs={{0,1},{1,2},{2,3},{3,0},{4,5},{5,6},{6,7},{7,4},{8,9},{9,10},{10,1... | collective-permute-start | bytes 1572872 | tf_op jit(solution)/shard_map/ppermute | solution.py:148
  26.0 1.1 collective-permute-start.7
  27.1 0.6 collective-permute-start.5
  27.7 0.0 copy-done.7
  27.7 0.1 fusion
  27.8 1.0 convert_reduce_fusion
  28.8 0.0 copy-start.8
  28.8 0.0 copy-start.9
  29.5 0.7 pad_add_fusion.1.meta_ref
  30.2 10.0 %collective-permute-done.3.q_ref = bf16[128,2048]{1,0:T(8,128)(2,1)S(1)} collective-permute-done((bf16[128,2048]{1,0:T(8,128)(2,1)}, bf16[128,2048]{1,0:T(8,128)(2,1)S(1)}, u32[]{:S(2)}, u32[]{:S(2)}) %collective-permute-start.3) | collective-permute-done | bytes 524320 | tf_op jit(solution)/shard_map/ppermute | solution.py:148
  40.2 19.2 %all-gather.2.cloned.1.call-done.k_ref.v_ref = bf16[4096,512]{1,0:T(8,128)(2,1)} async-done(((bf16[512,512]{1,0:T(8,128)(2,1)}), bf16[4096,512]{1,0:T(8,128)(2,1)}) %all-gather.2.cloned.1.call-update) | async-done | bytes 4194320 | tf_op jit(solution)/shard_map/all_gather | solution.py:132
  59.5 5.7 %shard_map.47 = bf16[128,2048]{1,0:T(8,128)(2,1)} custom-call(s32[3]{0:T(128)} %pad_add_fusion.1.meta_ref, s32[4096]{0:T(1024)} %doc_ref.7, bf16[128,2048]{1,0:T(8,128)(2,1)} %copy-done.6, bf16[4096,512]{1,0:T(8,128)(2,1)} %all-gather.2.cloned.1.call-done.k_ref.v_ref, bf16[4096,512]{1,0:T(8,128)(2,1)} %all-gather.2.cloned.1.call-done.k_ref.v_ref, ...), custom_call_target="tpu_custom_call" | custom-call | tf_op jit(solution)/shard_map/pallas_call | solution.py:94
  65.1 0.0 copy-done.9
  65.1 14.3 %collective-permute-start.4 = (bf16[128,2048]{1,0:T(8,128)(2,1)}, bf16[128,2048]{1,0:T(8,128)(2,1)S(1)}, u32[]{:S(2)}, u32[]{:S(2)}) collective-permute-start(bf16[128,2048]{1,0:T(8,128)(2,1)} %shard_map.47), channel_id=1, source_target_pairs={{0,3},{1,0},{2,1},{3,2},{4,7},{5,4},{6,5},{7,6},{8,11},{9,8},{10,9... | collective-permute-start | bytes 1572872 | tf_op jit(solution)/shard_map/ppermute | solution.py:152
  79.4 0.6 pad_add_fusion.3.meta_ref
  80.0 0.6 pad_add_fusion.2.meta_ref
  80.7 0.0 collective-permute-done.5.q_ref
  80.7 0.8 copy-done.5
  81.5 16.4 %shard_map.48 = bf16[128,2048]{1,0:T(8,128)(2,1)} custom-call(s32[3]{0:T(128)} %pad_add_fusion.2.meta_ref, s32[4096]{0:T(1024)} %doc_ref.7, bf16[128,2048]{1,0:T(8,128)(2,1)} %copy-done.5, bf16[4096,512]{1,0:T(8,128)(2,1)} %all-gather.2.cloned.1.call-done.k_ref.v_ref, bf16[4096,512]{1,0:T(8,128)(2,1)} %all-gather.2.cloned.1.call-done.k_ref.v_ref, ...), custom_call_target="tpu_custom_call" | custom-call | tf_op jit(solution)/shard_map/pallas_call | solution.py:94
  97.9 0.0 collective-permute-start.6
  97.9 0.6 pad_add_fusion.meta_ref
  98.5 0.0 collective-permute-done.7.q_ref
  98.5 0.8 copy-done.4
  99.3 15.5 %shard_map.49 = bf16[128,2048]{1,0:T(8,128)(2,1)} custom-call(s32[3]{0:T(128)} %pad_add_fusion.3.meta_ref, s32[4096]{0:T(1024)} %doc_ref.7, bf16[128,2048]{1,0:T(8,128)(2,1)} %copy-done.4, bf16[4096,512]{1,0:T(8,128)(2,1)} %all-gather.2.cloned.1.call-done.k_ref.v_ref, bf16[4096,512]{1,0:T(8,128)(2,1)} %all-gather.2.cloned.1.call-done.k_ref.v_ref, ...), custom_call_target="tpu_custom_call" | custom-call | tf_op jit(solution)/shard_map/pallas_call | solution.py:94
  114.8 0.6 collective-permute-start.8
  115.4 15.5 %shard_map.46 = bf16[128,2048]{1,0:T(8,128)(2,1)} custom-call(s32[3]{0:T(128)} %pad_add_fusion.meta_ref, s32[4096]{0:T(1024)} %doc_ref.7, bf16[128,2048]{1,0:T(8,128)(2,1)} %get-tuple-element.11.q_ref, bf16[4096,512]{1,0:T(8,128)(2,1)} %all-gather.2.cloned.1.call-done.k_ref.v_ref, bf16[4096,512]{1,0:T(8,128)(2,1)} %all-gather.2.cloned.1.call-done.k_ref.v_ref, ...), custom_call_target="tpu_custom_call" | custom-call | tf_op jit(solution)/shard_map/pallas_call | solution.py:94
  130.9 0.2 broadcast_in_dim.4
  131.1 0.8 copy-done.1
  132.0 0.0 collective-permute-done.4
  132.0 0.0 collective-permute-done.6
  132.1 0.0 copy-start
  132.1 0.0 collective-permute-done.8
  132.1 1.3 copy-done
  133.4 0.8 constant_dynamic-update-slice_fusion
  (22 shorter events, 0.3 us)
Async XLA Ops:
  6.5 52.9 %all-gather.2.cloned.1.call-start = ((), (), s32[]{:S(2)}) async-start(), calls=%async_computation | async-start | bytes 4718592 | tf_op jit(solution)/shard_map/all_gather | solution.py:132
  6.5 15.1 %copy-start.3 = (bf16[128,8192]{1,0:T(8,128)(2,1)S(1)}, bf16[128,8192]{1,0:T(8,128)(2,1)}, u32[]{:S(2)}) copy-start(bf16[128,8192]{1,0:T(8,128)(2,1)} %param.4) | copy-start | bytes 6291460
  7.8 8.3 %collective-permute-start = (bf16[128,512]{1,0:T(8,128)(2,1)S(1)}, bf16[128,512]{1,0:T(8,128)(2,1)S(1)}, u32[]{:S(2)}, u32[]{:S(2)}) collective-permute-start(bf16[128,512]{1,0:T(8,128)(2,1)S(1)} %pad_maximum_fusion), channel_id=1, source_target_pairs={{0,1},{1,2},{2,3},{3,0},{4,5},{5,6},{6,7},{7,4},{8,9},{9,10},{10,1... | collective-permute-start | bytes 393224 | tf_op jit(solution)/shard_map/ppermute | solution.py:130
  9.5 11.2 %collective-permute-start.1 = (bf16[128,512]{1,0:T(8,128)(2,1)S(1)}, bf16[128,512]{1,0:T(8,128)(2,1)S(1)}, u32[]{:S(2)}, u32[]{:S(2)}) collective-permute-start(bf16[128,512]{1,0:T(8,128)(2,1)S(1)} %pad_maximum_fusion.1), channel_id=1, source_target_pairs={{0,2},{1,3},{2,0},{3,1},{4,6},{5,7},{6,4},{7,5},{8,10},{9,11},{10,... | collective-permute-start | bytes 393224 | tf_op jit(solution)/shard_map/ppermute | solution.py:130
  12.1 8.6 %collective-permute-start.2 = (bf16[128,512]{1,0:T(8,128)(2,1)S(1)}, bf16[128,512]{1,0:T(8,128)(2,1)S(1)}, u32[]{:S(2)}, u32[]{:S(2)}) collective-permute-start(bf16[128,512]{1,0:T(8,128)(2,1)S(1)} %pad_maximum_fusion.2), channel_id=1, source_target_pairs={{0,3},{1,0},{2,1},{3,2},{4,7},{5,4},{6,5},{7,6},{8,11},{9,8},{10,9... | collective-permute-start | bytes 393224 | tf_op jit(solution)/shard_map/ppermute | solution.py:130
  20.7 0.8 copy-start.2
  21.6 6.1 %copy-start.7 = (s32[4096]{0:T(1024)S(1)}, s32[4096]{0:T(1024)}, u32[]{:S(2)}) copy-start(s32[4096]{0:T(1024)} %doc_ref.7) | copy-start | bytes 49156
  22.8 17.4 %collective-permute-start.3 = (bf16[128,2048]{1,0:T(8,128)(2,1)}, bf16[128,2048]{1,0:T(8,128)(2,1)S(1)}, u32[]{:S(2)}, u32[]{:S(2)}) collective-permute-start(bf16[128,2048]{1,0:T(8,128)(2,1)} %get-tuple-element.10), channel_id=1, source_target_pairs={{0,1},{1,2},{2,3},{3,0},{4,5},{5,6},{6,7},{7,4},{8,9},{9,10},{10,1... | collective-permute-start | bytes 1572872 | tf_op jit(solution)/shard_map/ppermute | solution.py:148
  26.0 72.5 %collective-permute-start.7 = (bf16[128,2048]{1,0:T(8,128)(2,1)S(1)}, bf16[128,2048]{1,0:T(8,128)(2,1)S(1)}, u32[]{:S(2)}, u32[]{:S(2)}) collective-permute-start(bf16[128,2048]{1,0:T(8,128)(2,1)S(1)} %get-tuple-element.9), channel_id=1, source_target_pairs={{0,3},{1,0},{2,1},{3,2},{4,7},{5,4},{6,5},{7,6},{8,11},{9,8},{10,9... | collective-permute-start | bytes 1572872 | tf_op jit(solution)/shard_map/ppermute | solution.py:148
  27.1 53.5 %collective-permute-start.5 = (bf16[128,2048]{1,0:T(8,128)(2,1)S(1)}, bf16[128,2048]{1,0:T(8,128)(2,1)S(1)}, u32[]{:S(2)}, u32[]{:S(2)}) collective-permute-start(bf16[128,2048]{1,0:T(8,128)(2,1)S(1)} %get-tuple-element.12), channel_id=1, source_target_pairs={{0,2},{1,3},{2,0},{3,1},{4,6},{5,7},{6,4},{7,5},{8,10},{9,11},{10,... | collective-permute-start | bytes 1572872 | tf_op jit(solution)/shard_map/ppermute | solution.py:148
  28.8 30.7 %copy-start.11 = (s32[128]{0:T(128)}, s32[128]{0:T(128)S(1)}, u32[]{:S(2)}) copy-start(s32[128]{0:T(128)S(1)} %get-tuple-element.6) | copy-start | bytes 1540
  28.8 36.3 %copy-start.8 = (s32[128]{0:T(128)}, s32[128]{0:T(128)S(1)}, u32[]{:S(2)}) copy-start(s32[128]{0:T(128)S(1)} %get-tuple-element.8) | copy-start | bytes 1540
  28.8 36.3 %copy-start.9 = (s32[128]{0:T(128)}, s32[128]{0:T(128)S(1)}, u32[]{:S(2)}) copy-start(s32[128]{0:T(128)S(1)} %get-tuple-element.5) | copy-start | bytes 1540
  28.8 36.3 %copy-start.10 = (s32[128]{0:T(128)}, s32[128]{0:T(128)S(1)}, u32[]{:S(2)}) copy-start(s32[128]{0:T(128)S(1)} %get-tuple-element.7) | copy-start | bytes 1540
  40.2 19.2 %copy-start.6 = (bf16[128,2048]{1,0:T(8,128)(2,1)}, bf16[128,2048]{1,0:T(8,128)(2,1)S(1)}, u32[]{:S(2)}) copy-start(bf16[128,2048]{1,0:T(8,128)(2,1)S(1)} %collective-permute-done.3.q_ref) | copy-start | bytes 1572868
  65.1 66.9 %collective-permute-start.4 = (bf16[128,2048]{1,0:T(8,128)(2,1)}, bf16[128,2048]{1,0:T(8,128)(2,1)S(1)}, u32[]{:S(2)}, u32[]{:S(2)}) collective-permute-start(bf16[128,2048]{1,0:T(8,128)(2,1)} %shard_map.47), channel_id=1, source_target_pairs={{0,3},{1,0},{2,1},{3,2},{4,7},{5,4},{6,5},{7,6},{8,11},{9,8},{10,9... | collective-permute-start | bytes 1572872 | tf_op jit(solution)/shard_map/ppermute | solution.py:152
  80.7 0.8 copy-start.5
  97.9 34.2 %collective-permute-start.6 = (bf16[128,2048]{1,0:T(8,128)(2,1)}, bf16[128,2048]{1,0:T(8,128)(2,1)S(1)}, u32[]{:S(2)}, u32[]{:S(2)}) collective-permute-start(bf16[128,2048]{1,0:T(8,128)(2,1)} %shard_map.48), channel_id=1, source_target_pairs={{0,2},{1,3},{2,0},{3,1},{4,6},{5,7},{6,4},{7,5},{8,10},{9,11},{10,... | collective-permute-start | bytes 1572872 | tf_op jit(solution)/shard_map/ppermute | solution.py:152
  98.5 0.8 copy-start.4
  114.8 17.3 %collective-permute-start.8 = (bf16[128,2048]{1,0:T(8,128)(2,1)}, bf16[128,2048]{1,0:T(8,128)(2,1)S(1)}, u32[]{:S(2)}, u32[]{:S(2)}) collective-permute-start(bf16[128,2048]{1,0:T(8,128)(2,1)} %shard_map.49), channel_id=1, source_target_pairs={{0,1},{1,2},{2,3},{3,0},{4,5},{5,6},{6,7},{7,4},{8,9},{9,10},{10,1... | collective-permute-start | bytes 1572872 | tf_op jit(solution)/shard_map/ppermute | solution.py:152
  130.9 1.0 copy-start.1
  132.1 1.3 copy-start
Sparse Core Ops, SparseCore 0:
  21.7 37.7 all-gather.1
